TPU v7x, 128 devices: a whole 4x4x4 slice. The times are simulated.
128 devices in a mesh: wave: 8 (over z_lo, x), strip: 16 (over y, z_hi, core).
Axes of the slice: x: 4, y: 4, z: 4 (z_hi: 2, z_lo: 2; z = z_hi * 2 + z_lo), core: 2. Of those that a mesh axis runs over, the one named last changes fastest.
Arguments:
- unit_params: float32 [9, 16, 24576], P(None, 'strip', 'wave'), may hold values from 0 to 1
- observed: bfloat16 [4, 256, 1536, 256], P(None, 'wave', 'strip'), may hold values from -3 to 3
- psf_rows: bfloat16 [256, 4, 65], P('wave'), may hold values from -0.75 to 0.75
- psf_cols: bfloat16 [256, 4, 65], P('wave'), may hold values from -0.75 to 0.75
- pixel_mask: int32 [1536, 256], P('strip'), may hold values 0 or 1
- strip_lengths: int32 [16], P('strip'), may hold values from 32 to 96, as said below
Outputs:
- param_grad: float32 [9, 16, 24576], P(None, 'strip', 'wave')
Inputs may be any that keep to these rules, and one draw needn't show every extreme that they name: `strip_lengths`: the strip lengths sum to 1024; in every draw one strip holds 96 rows and one holds 32.
All inputs are finite; a program needn't handle non-finite values. No bound on the sum of `pixel_mask` on one device may be relied on, other than what follows from the above.
Results may differ from a plain program's by a relative error of at most 0.00098.
Values may be sent and summed in bfloat16 or wider, within the bound.
No kernel may reach another device: no remote copies, remote signals or barrier semaphores. Data moves between devices by JAX's collectives and lax.ppermute only.
A program may use at most 192 MiB of HBM per device.

v0:
```python
import jax
import jax.numpy as jnp
from jax import lax
from jax.sharding import PartitionSpec as P

parameter_low = (0.2, 0.4, 2.0, -0.8, 0.4, 0.3, 0.0, 0.0, 0.0)
parameter_span = (0.4, 0.6, 18.0, 1.6, 0.8, 1.2, 1.5, 3.141592653589793, 3.141592653589793)
stokes_weight = (1.0, 3.0, 3.0, 2.0)
loss_scale = 0.03125


def passed_along(shard, axis, by):
    count = lax.axis_size(axis)
    pairs = [(i, i + by) for i in range(count) if 0 <= i + by < count]
    return lax.ppermute(shard, axis, pairs)


def profile(distance, damping):
    scaled = distance / damping
    return 1.0 / (1.0 + scaled * scaled)


def stokes_model(unit_params, wave_grid):
    physical = [
        parameter_low[number] + parameter_span[number] * unit_params[number] for number in range(9)
    ]
    (
        source_zero,
        source_slope,
        strength,
        doppler,
        line_width,
        damping,
        zeeman_split,
        incline,
        azimuth,
    ) = physical
    offset = (wave_grid[:, None, None] - doppler) / line_width
    split_ratio = zeeman_split / line_width
    centre = profile(offset, damping)
    upper_line = profile(offset - split_ratio, damping)
    lower_line = profile(offset + split_ratio, damping)
    cosine = jnp.cos(incline)
    sine_value = jnp.sin(incline)
    sine_square = sine_value * sine_value
    absorb_total = 1.0 + strength * (
        centre * sine_square * 0.5 + (upper_line + lower_line) * (1.0 + cosine * cosine) * 0.25
    )
    linear = strength * (centre - 0.5 * (upper_line + lower_line)) * sine_square * 0.5
    linear_cosine = linear * jnp.cos(2.0 * azimuth)
    linear_sine = linear * jnp.sin(2.0 * azimuth)
    circular = strength * (lower_line - upper_line) * cosine * 0.5
    denominator = (
        absorb_total * absorb_total
        - linear_cosine * linear_cosine
        - linear_sine * linear_sine
        - circular * circular
    )
    source_ratio = source_slope / denominator
    return jnp.stack(
        [
            source_zero + source_ratio * absorb_total,
            -source_ratio * linear_cosine,
            -source_ratio * linear_sine,
            -source_ratio * circular,
        ]
    )


def band_tables(tap_table, out_rows, tap_count):
    in_rows = out_rows + tap_count - 1
    target_row = lax.broadcasted_iota(jnp.int32, (out_rows, in_rows, tap_count), 0)
    source_row = lax.broadcasted_iota(jnp.int32, (out_rows, in_rows, tap_count), 1)
    tap_index = lax.broadcasted_iota(jnp.int32, (out_rows, in_rows, tap_count), 2)
    selector = (source_row - target_row == tap_index).astype(jnp.bfloat16)
    return jnp.einsum(
        "wkt,ijt->wkij", tap_table, selector, preferred_element_type=jnp.float32
    ).astype(jnp.bfloat16)


def column_tables(tap_table, columns, tap_count):
    radius = tap_count // 2
    source_column = lax.broadcasted_iota(jnp.int32, (columns, columns, tap_count), 0)
    target_column = lax.broadcasted_iota(jnp.int32, (columns, columns, tap_count), 1)
    tap_index = lax.broadcasted_iota(jnp.int32, (columns, columns, tap_count), 2)
    selector = (source_column - target_column + radius == tap_index).astype(jnp.bfloat16)
    return jnp.einsum(
        "wkt,xyt->wkxy", tap_table, selector, preferred_element_type=jnp.float32
    ).astype(jnp.bfloat16)


def extend(upper_rim, middle, lower_rim, length, axis_index):
    radius = upper_rim.shape[axis_index]
    widened = jnp.concatenate([upper_rim, middle, jnp.zeros_like(upper_rim)], axis=axis_index)
    return lax.dynamic_update_slice_in_dim(widened, lower_rim, radius + length, axis_index)


def per_device(unit_params, observed, psf_rows, psf_cols, pixel_mask, strip_lengths):
    stokes_count, wave_count, capacity, columns = observed.shape
    tap_count = psf_rows.shape[2]
    radius = tap_count // 2
    gathered = lax.all_gather(unit_params, "wave", axis=2, tiled=True)
    own_params = gathered.reshape(gathered.shape[0], capacity, columns)
    length = strip_lengths[0]
    wave_pos = lax.axis_index("wave")
    levels = (wave_pos * wave_count + jnp.arange(wave_count, dtype=jnp.int32)).astype(jnp.float32)
    wave_grid = -3.0 + 6.0 * levels / (wave_count * lax.axis_size("wave") - 1)
    row_index = jnp.arange(capacity, dtype=jnp.int32)
    rows_live = (row_index < length).astype(jnp.float32)
    model_own = (stokes_model(own_params, wave_grid) * rows_live[:, None]).astype(jnp.bfloat16)
    tail_rows = lax.dynamic_slice_in_dim(model_own, length - radius, radius, 2)
    upper_rim = passed_along(tail_rows, "strip", 1)
    lower_rim = passed_along(model_own[:, :, :radius], "strip", -1)
    model_wide = extend(upper_rim, model_own, lower_rim, length, 2)
    row_band = band_tables(psf_rows, capacity, tap_count)
    column_band = column_tables(psf_cols, columns, tap_count)
    live_mask = pixel_mask.astype(jnp.float32) * rows_live[:, None]
    weight_square = jnp.array(stokes_weight, jnp.float32)
    weight_square = weight_square * weight_square
    block_size = 4
    block_count = wave_count // block_size

    def forward(number, residual_all):
        first_wave = number * block_size
        model_block = lax.dynamic_slice_in_dim(model_wide, first_wave, block_size, 1)
        band_block = lax.dynamic_slice_in_dim(row_band, first_wave, block_size, 0)
        column_block = lax.dynamic_slice_in_dim(column_band, first_wave, block_size, 0)
        observed_block = lax.dynamic_slice_in_dim(observed, first_wave, block_size, 1)
        row_pass = jnp.einsum(
            "wkij,swjc->kswic", band_block, model_block, preferred_element_type=jnp.float32
        ).astype(jnp.bfloat16)
        blurred = jnp.einsum(
            "kswic,wkcd->swid", row_pass, column_block, preferred_element_type=jnp.float32
        )
        residual = (
            loss_scale
            * weight_square[:, None, None, None]
            * live_mask
            * (blurred - observed_block.astype(jnp.float32))
        ).astype(jnp.bfloat16)
        return lax.dynamic_update_slice_in_dim(residual_all, residual, first_wave, 1)

    residual_all = lax.fori_loop(0, block_count, forward, jnp.zeros(observed.shape, jnp.bfloat16))
    row_back = band_tables(psf_rows[:, :, ::-1], capacity, tap_count)
    tail_residual = lax.dynamic_slice_in_dim(residual_all, length - radius, radius, 2)
    upper_resid = passed_along(tail_residual, "strip", 1)
    lower_resid = passed_along(residual_all[:, :, :radius], "strip", -1)
    residual_wide = extend(upper_resid, residual_all, lower_resid, length, 2)

    def backward(number, gradient_sum):
        first_wave = number * block_size
        residual_block = lax.dynamic_slice_in_dim(residual_wide, first_wave, block_size, 1)
        column_block = lax.dynamic_slice_in_dim(column_band, first_wave, block_size, 0)
        back_block = lax.dynamic_slice_in_dim(row_back, first_wave, block_size, 0)
        grid_block = lax.dynamic_slice_in_dim(wave_grid, first_wave, block_size, 0)
        across = jnp.einsum(
            "swjc,wkdc->kswjd", residual_block, column_block, preferred_element_type=jnp.float32
        ).astype(jnp.bfloat16)
        adjoint = (
            jnp.einsum("wkij,kswjc->swic", back_block, across, preferred_element_type=jnp.float32)
            * rows_live[:, None]
        )

        def model_of(params_now):
            return stokes_model(params_now, grid_block)

        unused_model, pullback = jax.vjp(model_of, own_params)
        return gradient_sum + pullback(adjoint)[0]

    gradient_local = lax.fori_loop(
        0, block_count, backward, jnp.zeros(own_params.shape, jnp.float32)
    )
    gradient_flat = gradient_local.reshape(gathered.shape)
    gradient_total = lax.psum(gradient_flat, "wave")
    share_width = unit_params.shape[2]
    return lax.dynamic_slice_in_dim(gradient_total, wave_pos * share_width, share_width, 2)


def solution(mesh):
    return jax.shard_map(
        per_device,
        mesh=mesh,
        in_specs=(
            P(None, "strip", "wave"),
            P(None, "wave", "strip", None),
            P("wave", None, None),
            P("wave", None, None),
            P("strip", None),
            P("strip"),
        ),
        out_specs=P(None, "strip", "wave"),
        check_vma=False,
    )
```

profile of v0, /device:TPU:78, one launch (start us, length us, event | category | flops | bytes accessed | tf_op | source)
XLA Modules:
  0.0 507.7 jit_solution(6636742498582574275)
XLA Ops:
  6.5 30.1 %all_gather.3 = f32[9,1,24576]{2,1,0:T(1,128)S(1)} all-gather(f32[9,1,3072]{2,1,0:T(1,128)} %param.11), channel_id=1, replica_groups=mesh['wave'=8,'strip'=16] {'wave'}, dimensions={2}, use_global_device_ids=true | all-gather | bytes 995328 | tf_op jit(solution)/shard_map/all_gather | solution.py:102
  36.7 9.9 %fusion.103 = (f32[24576]{0:T(1024)S(1)}, f32[24576]{0:T(1024)S(1)}, f32[24576]{0:T(1024)S(1)}, f32[24576]{0:T(1024)S(1)}, f32[24576]{0:T(1024)S(1)}, /*index=5*...) fusion(f32[9,1,24576]{2,1,0:T(1,128)S(1)} %all_gather.3), kind=kLoop, calls=%fused_computation.198 | loop fusion | flops 442368 | bytes 1966080 | tf_op jit(solution)/shard_map/add | solution.py:25
  47.8 5.3 %multiply_add_fusion.8 = (f32[1,32,96,256]{3,2,1,0:T(8,128)S(1)}, f32[1,32,96,256]{3,2,1,0:T(8,128)S(1)}, f32[1,32,96,256]{3,2,1,0:T(8,128)S(1)}, f32[1,32,96,256]{3,2,1,0:T(8,128)S(1)}) fusion(f32[96,256]{1,0:T(8,128)S(1)} %get-tuple-element.546, f32[96,256]{1,0:T(8,128)S(1)} %add.585, f32[96,256]{1,0:T(8,128)S(1)} %get-tuple-element.545, ...), kind=kLoop, calls=%fused_computation.166 | loop fusion | flops 37748736 | bytes 13860992 | tf_op jit(solution)/shard_map/add | solution.py:62
  61.0 5.3 %collective-permute-start.1 = (bf16[4,32,32,256]{3,2,1,0:T(8,128)(2,1)}, bf16[4,32,32,256]{3,2,1,0:T(8,128)(2,1)}, u32[]{:S(2)}, u32[]{:S(2)}) collective-permute-start(bf16[4,32,32,256]{3,2,1,0:T(8,128)(2,1)} %get-tuple-element.538), channel_id=1, source_target_pairs={{1,0},{2,1},{3,2},{4,3},{5,4},{6,5},{7,6},{8,7},{9,8},{10,9},{11,1... | collective-permute-start | bytes 6291464 | tf_op jit(solution)/shard_map/ppermute | solution.py:15
  66.3 8.5 %convert_bitcast_fusion = bf16[32,4,256,256]{3,0,1,2:T(8,128)(2,1)} fusion(bf16[32,4,65]{2,1,0:T(4,128)(2,1)S(1)} %copy-done.4), kind=kOutput, calls=%fused_computation.149 | convolution fusion | flops 1111687168 | bytes 16793856 | tf_op jit(solution)/shard_map/wkt,xyt->wkxy/dot_general | solution.py:87
  74.8 16.3 %copy.20 = bf16[32,4,256,256]{3,2,1,0:T(8,128)(2,1)} copy(bf16[32,4,256,256]{3,0,1,2:T(8,128)(2,1)} %convert_bitcast_fusion) | data formatting | bytes 33554432
  95.1 15.6 %collective-permute-done = bf16[4,32,32,256]{3,2,1,0:T(8,128)(2,1)} collective-permute-done((bf16[4,32,32,256]{3,2,1,0:T(8,128)(2,1)}, bf16[4,32,32,256]{3,2,1,0:T(8,128)(2,1)}, u32[]{:S(2)}, u32[]{:S(2)}) %collective-permute-start) | collective-permute-done | bytes 2097184 | tf_op jit(solution)/shard_map/ppermute | solution.py:15
  110.7 10.1 %maximum_maximum_fusion = bf16[4,32,160,256]{3,2,1,0:T(8,128)(2,1)} fusion(bf16[4,32,96,256]{3,2,1,0:T(8,128)(2,1)} %copy-done.1, bf16[4,32,32,256]{3,2,1,0:T(8,128)(2,1)} %collective-permute-done, bf16[160]{0:T(256)(128)(2,1)S(1)} %pad.113.clone), kind=kLoop, calls=%fused_computation.152 | loop fusion | flops 31457280 | bytes 18874688 | tf_op jit(solution)/shard_map/concatenate | solution.py:94
  120.7 20.6 %dynamic_update_slice.13 = bf16[4,32,160,256]{3,2,1,0:T(8,128)(2,1)} dynamic-update-slice(bf16[4,32,160,256]{3,2,1,0:T(8,128)(2,1)} %maximum_maximum_fusion, bf16[4,32,32,256]{3,2,1,0:T(8,128)(2,1)} %collective-permute-done.1, s32[]{:T(128)} %constant.278.clone.1, s32[]{:T(128)} %constant.278.clone.1, s32[]{:T(128)S(6)} %select_n.37, s32[]{:T(128)} %constant.278.clone.1) | dynamic-update-slice | bytes 4194308 | tf_op jit(solution)/shard_map/dynamic_update_slice | solution.py:95
  144.7 58.5 %while.31 = (s32[]{:T(128)}, bf16[4,32,96,256]{3,2,1,0:T(8,128)(2,1)}, f32[96,256]{1,0:T(8,128)S(1)}, bf16[32,4,256,256]{3,2,1,0:T(8,128)(2,1)}, bf16[4,32,160,2...) while((s32[]{:T(128)}, ...), condition=%wide.region_1.0_spmd.clone, body=%wide.region_0.0_spmd.clone.sunk | while | flops 1311866880 | bytes 9897691 | solution.py:143
  147.1 4.0 fusion.130
  154.4 4.0 fusion.130
  169.0 4.0 fusion.130
  176.3 4.0 fusion.130
  183.6 4.0 fusion.130
  198.2 4.0 fusion.130
  203.2 5.5 %fusion.112 = (bf16[4,32,32,256]{3,2,1,0:T(8,128)(2,1)}, bf16[4,32,32,256]{3,2,1,0:T(8,128)(2,1)}) fusion(bf16[4,32,96,256]{3,2,1,0:T(8,128)(2,1)} %get-tuple-element.364, s32[]{:T(128)S(6)} %select_n.36), kind=kLoop, calls=%fused_computation.217 | loop fusion | bytes 8388612 | tf_op jit(solution)/shard_map/slice | solution.py:147
  210.6 5.4 %collective-permute-start.3 = (bf16[4,32,32,256]{3,2,1,0:T(8,128)(2,1)}, bf16[4,32,32,256]{3,2,1,0:T(8,128)(2,1)}, u32[]{:S(2)}, u32[]{:S(2)}) collective-permute-start(bf16[4,32,32,256]{3,2,1,0:T(8,128)(2,1)} %get-tuple-element.536), channel_id=1, source_target_pairs={{1,0},{2,1},{3,2},{4,3},{5,4},{6,5},{7,6},{8,7},{9,8},{10,9},{11,1... | collective-permute-start | bytes 6291464 | tf_op jit(solution)/shard_map/ppermute | solution.py:15
  221.6 4.0 convert_bitcast_fusion.1
  225.6 34.0 %collective-permute-done.2 = bf16[4,32,32,256]{3,2,1,0:T(8,128)(2,1)} collective-permute-done((bf16[4,32,32,256]{3,2,1,0:T(8,128)(2,1)}, bf16[4,32,32,256]{3,2,1,0:T(8,128)(2,1)}, u32[]{:S(2)}, u32[]{:S(2)}) %collective-permute-start.2) | collective-permute-done | bytes 2097184 | tf_op jit(solution)/shard_map/ppermute | solution.py:15
  259.6 7.9 %maximum_maximum_fusion.1 = bf16[4,32,160,256]{3,2,1,0:T(8,128)(2,1)} fusion(bf16[4,32,96,256]{3,2,1,0:T(8,128)(2,1)S(1)} %copy-done, bf16[4,32,32,256]{3,2,1,0:T(8,128)(2,1)} %collective-permute-done.2, bf16[160]{0:T(256)(128)(2,1)S(1)} %pad.113.clone), kind=kLoop, calls=%fused_computation.153 | loop fusion | flops 31457280 | bytes 18874688 | tf_op jit(solution)/shard_map/concatenate | solution.py:94
  267.5 20.6 %dynamic_update_slice.14 = bf16[4,32,160,256]{3,2,1,0:T(8,128)(2,1)} dynamic-update-slice(bf16[4,32,160,256]{3,2,1,0:T(8,128)(2,1)} %maximum_maximum_fusion.1, bf16[4,32,32,256]{3,2,1,0:T(8,128)(2,1)} %collective-permute-done.3, s32[]{:T(128)} %constant.278.clone.1, s32[]{:T(128)} %constant.278.clone.1, s32[]{:T(128)S(6)} %select_n.37, s32[]{:T(128)} %constant.278.clone.1) | dynamic-update-slice | bytes 4194308 | tf_op jit(solution)/shard_map/dynamic_update_slice | solution.py:95
  288.1 134.8 %while.32 = (s32[]{:T(128)}, f32[9,96,256]{2,1,0:T(8,128)S(1)}, f32[9,96,256]{2,1,0:T(8,128)S(1)}, f32[32]{0:T(128)S(1)}, bf16[32,4,256,256]{3,2,1,0:T(8,128)(2,...) while((s32[]{:T(128)}, f32[9,96,256]{2,1,0:T(8,128)S(1)}, ...), condition=%wide.region_21.22_spmd.clone, body=%wide.region_2.21_spmd.clone.sunk | while | flops 1872642304 | bytes 34342920 | solution.py:170
  291.3 4.9 fusion.134
  308.1 4.9 fusion.134
  325.0 4.9 fusion.134
  341.8 4.9 fusion.134
  358.7 4.9 fusion.134
  375.6 4.9 fusion.134
  392.4 4.9 fusion.134
  409.3 4.9 fusion.134
  424.8 74.5 %all-reduce.11.cloned.1.call-done = f32[9,1,24576]{2,1,0:T(1,128)} async-done(((f32[9,1,24576]{2,1,0:T(1,128)}), f32[9,1,24576]{2,1,0:T(1,128)}) %all-reduce.11.cloned.1.call-update) | async-done | bytes 884752 | tf_op jit(solution)/shard_map/psum | solution.py:174
  (208 shorter events, 156.2 us)
Async XLA Ops:
  6.5 492.7 %all-reduce.11.cloned.1.call-start = ((), (), s32[]{:S(2)}) async-start(), calls=%async_computation | async-start | bytes 1769472 | tf_op jit(solution)/shard_map/psum | solution.py:174
  55.1 3.9 copy-start.1
  55.1 11.2 %copy-start.4 = (bf16[32,4,65]{2,1,0:T(4,128)(2,1)S(1)}, bf16[32,4,65]{2,1,0:T(4,128)(2,1)}, u32[]{:S(2)}) copy-start(bf16[32,4,65]{2,1,0:T(4,128)(2,1)} %param.14) | copy-start | bytes 49924
  59.0 51.6 %collective-permute-start = (bf16[4,32,32,256]{3,2,1,0:T(8,128)(2,1)}, bf16[4,32,32,256]{3,2,1,0:T(8,128)(2,1)}, u32[]{:S(2)}, u32[]{:S(2)}) collective-permute-start(bf16[4,32,32,256]{3,2,1,0:T(8,128)(2,1)} %get-tuple-element.539), channel_id=1, source_target_pairs={{0,1},{1,2},{2,3},{3,4},{4,5},{5,6},{6,7},{7,8},{8,9},{9,10},{10,1... | collective-permute-start | bytes 6291464 | tf_op jit(solution)/shard_map/ppermute | solution.py:15
  61.0 59.8 %collective-permute-start.1 = (bf16[4,32,32,256]{3,2,1,0:T(8,128)(2,1)}, bf16[4,32,32,256]{3,2,1,0:T(8,128)(2,1)}, u32[]{:S(2)}, u32[]{:S(2)}) collective-permute-start(bf16[4,32,32,256]{3,2,1,0:T(8,128)(2,1)} %get-tuple-element.538), channel_id=1, source_target_pairs={{1,0},{2,1},{3,2},{4,3},{5,4},{6,5},{7,6},{8,7},{9,8},{10,9},{11,1... | collective-permute-start | bytes 6291464 | tf_op jit(solution)/shard_map/ppermute | solution.py:15
  74.8 16.4 %copy-start.3 = (s32[96,256]{1,0:T(8,128)S(1)}, s32[96,256]{1,0:T(8,128)}, u32[]{:S(2)}) copy-start(s32[96,256]{1,0:T(8,128)} %param.15) | copy-start | bytes 294916
  74.8 16.4 %copy-start.2 = (bf16[32,4,65]{2,1,0:T(4,128)(2,1)S(1)}, bf16[32,4,65]{2,1,0:T(4,128)(2,1)}, u32[]{:S(2)}) copy-start(bf16[32,4,65]{2,1,0:T(4,128)(2,1)} %param.13) | copy-start | bytes 49924
  141.3 3.4 copy-start.5
  208.7 51.0 %collective-permute-start.2 = (bf16[4,32,32,256]{3,2,1,0:T(8,128)(2,1)}, bf16[4,32,32,256]{3,2,1,0:T(8,128)(2,1)}, u32[]{:S(2)}, u32[]{:S(2)}) collective-permute-start(bf16[4,32,32,256]{3,2,1,0:T(8,128)(2,1)} %get-tuple-element.537), channel_id=1, source_target_pairs={{0,1},{1,2},{2,3},{3,4},{4,5},{5,6},{6,7},{7,8},{8,9},{9,10},{10,1... | collective-permute-start | bytes 6291464 | tf_op jit(solution)/shard_map/ppermute | solution.py:15
  210.6 56.9 %collective-permute-start.3 = (bf16[4,32,32,256]{3,2,1,0:T(8,128)(2,1)}, bf16[4,32,32,256]{3,2,1,0:T(8,128)(2,1)}, u32[]{:S(2)}, u32[]{:S(2)}) collective-permute-start(bf16[4,32,32,256]{3,2,1,0:T(8,128)(2,1)} %get-tuple-element.536), channel_id=1, source_target_pairs={{1,0},{2,1},{3,2},{4,3},{5,4},{6,5},{7,6},{8,7},{9,8},{10,9},{11,1... | collective-permute-start | bytes 6291464 | tf_op jit(solution)/shard_map/ppermute | solution.py:15
  221.6 38.1 %copy-start = (bf16[4,32,96,256]{3,2,1,0:T(8,128)(2,1)S(1)}, bf16[4,32,96,256]{3,2,1,0:T(8,128)(2,1)}, u32[]{:S(2)}) copy-start(bf16[4,32,96,256]{3,2,1,0:T(8,128)(2,1)} %get-tuple-element.364) | copy-start | bytes 18874372
Sparse Core Ops, SparseCore 0:
  424.9 74.3 all-reduce.10
where the time goes:
time: 514 us; the launch traced here: 508 us
  waiting for transfers between devices  124 us (24%)
  local copies, waits for them, and re-layouts  123 us (24%)
  other arithmetic  114 us (22%)
  matrix products  87 us (17%)
  blocking collectives  30.1 us (6%)
  starting transfers between devices  14.5 us (3%)
  between operations  14.3 us (3%)
    psum x1, waiting for transfers between devices, per_device(): gradient_total = lax.psum(gradient_flat, 'wave')  74.5 us
    ppermute x4, waiting for transfers between devices, passed_along(): return lax.ppermute(shard, axis, pairs)  49.6 us
    dynamic_update_slice x2, local copies, waits for them, and re-layouts, extend(): lax.dynamic_update_slice_in_dim(widened, lower_rim, radius + length, axis...  41.2 us
    dot_general x8, matrix products, backward(): jnp.einsum('wkij,kswjc->swic', back_block, across, preferred_element_type...  39.1 us
    dot_general x8, matrix products, forward(): jnp.einsum('kswic,wkcd->swid', row_pass, column_block, preferred_element_...  31.6 us
    all_gather x1, blocking collectives, per_device(): gathered = lax.all_gather(unit_params, 'wave', axis=2, tiled=True)  30.1 us
    mul x32, other arithmetic, stokes_model(): parameter_span[number] * unit_params[number]  22.7 us
    dynamic_slice x8, local copies, waits for them, and re-layouts, backward(): back_block = lax.dynamic_slice_in_dim(row_back, first_wave, block_size, 0)  20.2 us
  transfers between devices with their start and end apart: 5, of which 3 were waited for; matrix products, arithmetic and copies ran while one was open for 11% of the time, Pallas kernels for 0%

commit v1 on v0

--- a/solution.py
+++ b/solution.py
@@ -13,6 +13,42 @@
     count = lax.axis_size(axis)
     pairs = [(i, i + by) for i in range(count) if 0 <= i + by < count]
     return lax.ppermute(shard, axis, pairs)
+
+
+def exchange(shard, axis, bit):
+    count = lax.axis_size(axis)
+    pairs = [(i, i ^ bit) for i in range(count)]
+    return lax.ppermute(shard, axis, pairs)
+
+
+def gather_by_doubling(shard, axis):
+    count = lax.axis_size(axis)
+    position = lax.axis_index(axis)
+    bit = 1
+    while bit < count:
+        other = exchange(shard, axis, bit)
+        low_side = (position & bit) == 0
+        shard = jnp.where(
+            low_side,
+            jnp.concatenate([shard, other], axis=0),
+            jnp.concatenate([other, shard], axis=0),
+        )
+        bit *= 2
+    return shard
+
+
+def scatter_by_halving(pieces, axis):
+    count = lax.axis_size(axis)
+    position = lax.axis_index(axis)
+    bit = count // 2
+    while bit >= 1:
+        half = pieces.shape[0] // 2
+        high_side = ((position & bit) != 0).astype(jnp.int32)
+        keep = lax.dynamic_slice_in_dim(pieces, high_side * half, half, 0)
+        give = lax.dynamic_slice_in_dim(pieces, (1 - high_side) * half, half, 0)
+        pieces = keep + exchange(give, axis, bit)
+        bit //= 2
+    return pieces[0]
 
 
 def profile(distance, damping):
@@ -99,8 +135,13 @@
     stokes_count, wave_count, capacity, columns = observed.shape
     tap_count = psf_rows.shape[2]
     radius = tap_count // 2
-    gathered = lax.all_gather(unit_params, "wave", axis=2, tiled=True)
-    own_params = gathered.reshape(gathered.shape[0], capacity, columns)
+    wave_total = lax.axis_size("wave")
+    gathered = gather_by_doubling(unit_params.reshape(1, -1), "wave")
+    own_params = (
+        gathered.reshape(wave_total, unit_params.shape[0], capacity // wave_total, columns)
+        .transpose(1, 0, 2, 3)
+        .reshape(unit_params.shape[0], capacity, columns)
+    )
     length = strip_lengths[0]
     wave_pos = lax.axis_index("wave")
     levels = (wave_pos * wave_count + jnp.arange(wave_count, dtype=jnp.int32)).astype(jnp.float32)
@@ -170,10 +211,10 @@
     gradient_local = lax.fori_loop(
         0, block_count, backward, jnp.zeros(own_params.shape, jnp.float32)
     )
-    gradient_flat = gradient_local.reshape(gathered.shape)
-    gradient_total = lax.psum(gradient_flat, "wave")
-    share_width = unit_params.shape[2]
-    return lax.dynamic_slice_in_dim(gradient_total, wave_pos * share_width, share_width, 2)
+    pieces = gradient_local.reshape(
+        gradient_local.shape[0], wave_total, capacity // wave_total, columns
+    ).transpose(1, 0, 2, 3)
+    return scatter_by_halving(pieces, "wave").reshape(unit_params.shape)
 
 
 def solution(mesh):

time: 514 us -> 426 us (0.83)
  waiting for transfers between devices: 124 us -> 88.8 us
  blocking collectives: 30.1 us -> 0 us
  local copies, waits for them, and re-layouts: 123 us -> 107 us
  between operations: 14.3 us -> 1.04 us
  starting transfers between devices: 14.5 us -> 22.5 us
  matrix products: 87 us -> 94.7 us
  other arithmetic: 114 us -> 108 us
    psum x1 -> x0, waiting for transfers between devices: 74.5 us -> none  [per_device(): gradient_total = lax.psum(gradient_flat, 'wave')]
    ppermute x0 -> x6, waiting for transfers between devices: none -> 33.4 us  [exchange(): return lax.ppermute(shard, axis, pairs)]
    all_gather x1 -> x0, blocking collectives: 30.1 us -> none  [per_device(): gathered = lax.all_gather(unit_params, 'wave', axis=2, tiled=True)]
    add x1, other arithmetic: 9.95 us -> 1.05 us  [stokes_model(): parameter_low[number] + parameter_span[number] * unit_params[number]]
    ppermute x0 -> x6, starting transfers between devices: none -> 8 us  [exchange(): return lax.ppermute(shard, axis, pairs)]
    dot_general x8, matrix products: 31.6 us -> 39.4 us  [forward(): jnp.einsum('kswic,wkcd->swid', row_pass, column_block, preferred_element_...]
    dynamic_update_slice x8 -> x0, local copies, waits for them, and re-layouts: 7.64 us -> none  [forward(): lax.dynamic_update_slice_in_dim(residual_all, residual, first_wave, 1)]
    ppermute x4, waiting for transfers between devices: 49.6 us -> 55.4 us  [passed_along(): return lax.ppermute(shard, axis, pairs)]
  transfers between devices with their start and end apart: 5 -> 10, of which waited for: 3 -> 8; matrix products, arithmetic and copies ran while one was open for 11% -> 13% of each run, Pallas kernels for 0% -> 0%
where the time goes in v1:
time: 426 us; the launch traced here: 422 us
  other arithmetic  108 us (25%)
  local copies, waits for them, and re-layouts  107 us (25%)
  matrix products  94.7 us (22%)
  waiting for transfers between devices  88.8 us (21%)
  starting transfers between devices  22.5 us (5%)
    ppermute x4, waiting for transfers between devices, passed_along(): return lax.ppermute(shard, axis, pairs)  55.4 us
    dynamic_update_slice x2, local copies, waits for them, and re-layouts, extend(): lax.dynamic_update_slice_in_dim(widened, lower_rim, radius + length, axis...  40.8 us
    dot_general x8, matrix products, forward(): jnp.einsum('kswic,wkcd->swid', row_pass, column_block, preferred_element_...  39.4 us
    dot_general x8, matrix products, backward(): jnp.einsum('wkij,kswjc->swic', back_block, across, preferred_element_type...  39 us
    ppermute x6, waiting for transfers between devices, exchange(): return lax.ppermute(shard, axis, pairs)  33.4 us
    mul x32, other arithmetic, stokes_model(): parameter_span[number] * unit_params[number]  22.7 us
    dynamic_slice x8, local copies, waits for them, and re-layouts, backward(): back_block = lax.dynamic_slice_in_dim(row_back, first_wave, block_size, 0)  20.2 us
    concatenate x2, other arithmetic, extend(): jnp.concatenate([upper_rim, middle, jnp.zeros_like(upper_rim)], axis=axis...  20.2 us
  transfers between devices with their start and end apart: 10, of which 8 were waited for; matrix products, arithmetic and copies ran while one was open for 13% of the time, Pallas kernels for 0%

profile of v1, /device:TPU:78, one launch (start us, length us, event | category | flops | bytes accessed | tf_op | source)
XLA Modules:
  0.0 422.4 jit_solution(4539183497604790005)
XLA Ops:
  18.0 6.8 %collective-permute-done.2 = f32[4,27648]{1,0:T(4,128)S(1)} collective-permute-done((f32[4,27648]{1,0:T(4,128)S(1)}, f32[4,27648]{1,0:T(4,128)S(1)}, u32[]{:S(2)}, u32[]{:S(2)}) %collective-permute-start.2) | collective-permute-done | bytes 442400 | tf_op jit(solution)/shard_map/ppermute | solution.py:21
  26.6 5.3 %multiply_add_fusion.8 = (f32[1,32,96,256]{3,2,0,1:T(8,128)S(1)}, f32[1,32,96,256]{3,2,0,1:T(8,128)S(1)}, f32[1,32,96,256]{3,2,0,1:T(8,128)S(1)}, f32[1,32,96,256]{3,2,0,1:T(8,128)S(1)}) fusion(f32[96,256]{1,0:T(8,128)S(1)} %get-tuple-element.576, f32[96,256]{1,0:T(8,128)S(1)} %add.604, f32[96,256]{1,0:T(8,128)S(1)} %get-tuple-element.575, ...), kind=kLoop, calls=%fused_computation.166 | loop fusion | flops 37748736 | bytes 13860992 | tf_op jit(solution)/shard_map/add | solution.py:98
  39.9 5.3 %collective-permute-start.4 = (bf16[4,32,32,256]{3,2,0,1:T(8,128)(2,1)}, bf16[4,32,32,256]{3,2,0,1:T(8,128)(2,1)}, u32[]{:S(2)}, u32[]{:S(2)}) collective-permute-start(bf16[4,32,32,256]{3,2,0,1:T(8,128)(2,1)} %get-tuple-element.557), channel_id=1, source_target_pairs={{1,0},{2,1},{3,2},{4,3},{5,4},{6,5},{7,6},{8,7},{9,8},{10,9},{11,1... | collective-permute-start | bytes 6291464 | tf_op jit(solution)/shard_map/ppermute | solution.py:15
  45.2 8.5 %convert_bitcast_fusion = bf16[32,4,256,256]{3,0,1,2:T(8,128)(2,1)} fusion(bf16[32,4,65]{2,1,0:T(4,128)(2,1)S(1)} %copy-done.3), kind=kOutput, calls=%fused_computation.149 | convolution fusion | flops 1111687168 | bytes 16793856 | tf_op jit(solution)/shard_map/wkt,xyt->wkxy/dot_general | solution.py:123
  53.7 16.3 %copy.61 = bf16[32,4,256,256]{3,2,1,0:T(8,128)(2,1)} copy(bf16[32,4,256,256]{3,0,1,2:T(8,128)(2,1)} %convert_bitcast_fusion) | data formatting | bytes 33554432
  74.0 15.6 %collective-permute-done.3 = bf16[4,32,32,256]{3,2,0,1:T(8,128)(2,1)} collective-permute-done((bf16[4,32,32,256]{3,2,0,1:T(8,128)(2,1)}, bf16[4,32,32,256]{3,2,0,1:T(8,128)(2,1)}, u32[]{:S(2)}, u32[]{:S(2)}) %collective-permute-start.3) | collective-permute-done | bytes 2097184 | tf_op jit(solution)/shard_map/ppermute | solution.py:15
  89.6 10.1 %maximum_maximum_fusion = bf16[4,32,160,256]{3,2,0,1:T(8,128)(2,1)} fusion(bf16[4,32,96,256]{3,2,0,1:T(8,128)(2,1)} %copy-done, bf16[4,32,32,256]{3,2,0,1:T(8,128)(2,1)} %collective-permute-done.3, bf16[160]{0:T(256)(128)(2,1)S(1)} %pad.113.clone), kind=kLoop, calls=%fused_computation.152 | loop fusion | flops 31457280 | bytes 18874688 | tf_op jit(solution)/shard_map/concatenate | solution.py:130
  99.7 20.4 %dynamic_update_slice.13 = bf16[4,32,160,256]{3,2,0,1:T(8,128)(2,1)} dynamic-update-slice(bf16[4,32,160,256]{3,2,0,1:T(8,128)(2,1)} %maximum_maximum_fusion, bf16[4,32,32,256]{3,2,0,1:T(8,128)(2,1)} %collective-permute-done.4, s32[]{:T(128)} %constant.285.clone.1, s32[]{:T(128)} %constant.285.clone.1, s32[]{:T(128)S(6)} %select_n.93, s32[]{:T(128)} %constant.285.clone.1) | dynamic-update-slice | bytes 4194308 | tf_op jit(solution)/shard_map/dynamic_update_slice | solution.py:131
  123.4 53.5 %while.31 = (s32[]{:T(128)}, bf16[4,32,96,256]{3,2,0,1:T(8,128)(2,1)}, f32[96,256]{1,0:T(8,128)S(1)}, bf16[32,4,256,256]{3,2,1,0:T(8,128)(2,1)}, bf16[4,32,160,2...) while((s32[]{:T(128)}, ...), condition=%wide.region_1.2_spmd.clone, body=%wide.region_0.1_spmd.clone.sunk | while | flops 1311866880 | bytes 7342295 | solution.py:184
  125.2 4.9 %fusion.133 = bf16[4,32,96,256]{3,2,0,1:T(8,128)(2,1)} fusion(bf16[4,32,96,256]{3,2,0,1:T(8,128)(2,1)} %get-tuple-element.794, s32[]{:T(128)S(6)} %select_n.114, bf16[32,4,256,256]{3,2,1,0:T(8,128)(2,1)} %get-tuple-element.808, bf16[4,32,160,256]{3,2,0,1:T(8,128)(2,1)} %get-tuple-element.809, f32[4,96,256]{2,1,0:T(8,128)S(1)} %broadcast_multiply_fusion.11, ...), kind=kOutput, calls=%fused_computation.11.clone.1 | convolution fusion | flops 1311768576 | bytes 5867520 | tf_op jit(solution)/shard_map/while/body/eval_jaxpr/kswic,wkcd->swid/dot_general | solution.py:173
  131.9 4.9 %fusion.133 = bf16[4,32,96,256]{3,2,0,1:T(8,128)(2,1)} fusion(bf16[4,32,96,256]{3,2,0,1:T(8,128)(2,1)} %get-tuple-element.794, s32[]{:T(128)S(6)} %select_n.114, bf16[32,4,256,256]{3,2,1,0:T(8,128)(2,1)} %get-tuple-element.808, bf16[4,32,160,256]{3,2,0,1:T(8,128)(2,1)} %get-tuple-element.809, f32[4,96,256]{2,1,0:T(8,128)S(1)} %broadcast_multiply_fusion.11, ...), kind=kOutput, calls=%fused_computation.11.clone.1 | convolution fusion | flops 1311768576 | bytes 5867520 | tf_op jit(solution)/shard_map/while/body/eval_jaxpr/kswic,wkcd->swid/dot_general | solution.py:173
  138.5 4.9 %fusion.133 = bf16[4,32,96,256]{3,2,0,1:T(8,128)(2,1)} fusion(bf16[4,32,96,256]{3,2,0,1:T(8,128)(2,1)} %get-tuple-element.794, s32[]{:T(128)S(6)} %select_n.114, bf16[32,4,256,256]{3,2,1,0:T(8,128)(2,1)} %get-tuple-element.808, bf16[4,32,160,256]{3,2,0,1:T(8,128)(2,1)} %get-tuple-element.809, f32[4,96,256]{2,1,0:T(8,128)S(1)} %broadcast_multiply_fusion.11, ...), kind=kOutput, calls=%fused_computation.11.clone.1 | convolution fusion | flops 1311768576 | bytes 5867520 | tf_op jit(solution)/shard_map/while/body/eval_jaxpr/kswic,wkcd->swid/dot_general | solution.py:173
  145.2 5.0 %fusion.133 = bf16[4,32,96,256]{3,2,0,1:T(8,128)(2,1)} fusion(bf16[4,32,96,256]{3,2,0,1:T(8,128)(2,1)} %get-tuple-element.794, s32[]{:T(128)S(6)} %select_n.114, bf16[32,4,256,256]{3,2,1,0:T(8,128)(2,1)} %get-tuple-element.808, bf16[4,32,160,256]{3,2,0,1:T(8,128)(2,1)} %get-tuple-element.809, f32[4,96,256]{2,1,0:T(8,128)S(1)} %broadcast_multiply_fusion.11, ...), kind=kOutput, calls=%fused_computation.11.clone.1 | convolution fusion | flops 1311768576 | bytes 5867520 | tf_op jit(solution)/shard_map/while/body/eval_jaxpr/kswic,wkcd->swid/dot_general | solution.py:173
  152.0 4.9 %fusion.133 = bf16[4,32,96,256]{3,2,0,1:T(8,128)(2,1)} fusion(bf16[4,32,96,256]{3,2,0,1:T(8,128)(2,1)} %get-tuple-element.794, s32[]{:T(128)S(6)} %select_n.114, bf16[32,4,256,256]{3,2,1,0:T(8,128)(2,1)} %get-tuple-element.808, bf16[4,32,160,256]{3,2,0,1:T(8,128)(2,1)} %get-tuple-element.809, f32[4,96,256]{2,1,0:T(8,128)S(1)} %broadcast_multiply_fusion.11, ...), kind=kOutput, calls=%fused_computation.11.clone.1 | convolution fusion | flops 1311768576 | bytes 5867520 | tf_op jit(solution)/shard_map/while/body/eval_jaxpr/kswic,wkcd->swid/dot_general | solution.py:173
  158.7 4.9 %fusion.133 = bf16[4,32,96,256]{3,2,0,1:T(8,128)(2,1)} fusion(bf16[4,32,96,256]{3,2,0,1:T(8,128)(2,1)} %get-tuple-element.794, s32[]{:T(128)S(6)} %select_n.114, bf16[32,4,256,256]{3,2,1,0:T(8,128)(2,1)} %get-tuple-element.808, bf16[4,32,160,256]{3,2,0,1:T(8,128)(2,1)} %get-tuple-element.809, f32[4,96,256]{2,1,0:T(8,128)S(1)} %broadcast_multiply_fusion.11, ...), kind=kOutput, calls=%fused_computation.11.clone.1 | convolution fusion | flops 1311768576 | bytes 5867520 | tf_op jit(solution)/shard_map/while/body/eval_jaxpr/kswic,wkcd->swid/dot_general | solution.py:173
  165.3 4.9 %fusion.133 = bf16[4,32,96,256]{3,2,0,1:T(8,128)(2,1)} fusion(bf16[4,32,96,256]{3,2,0,1:T(8,128)(2,1)} %get-tuple-element.794, s32[]{:T(128)S(6)} %select_n.114, bf16[32,4,256,256]{3,2,1,0:T(8,128)(2,1)} %get-tuple-element.808, bf16[4,32,160,256]{3,2,0,1:T(8,128)(2,1)} %get-tuple-element.809, f32[4,96,256]{2,1,0:T(8,128)S(1)} %broadcast_multiply_fusion.11, ...), kind=kOutput, calls=%fused_computation.11.clone.1 | convolution fusion | flops 1311768576 | bytes 5867520 | tf_op jit(solution)/shard_map/while/body/eval_jaxpr/kswic,wkcd->swid/dot_general | solution.py:173
  172.0 4.9 %fusion.133 = bf16[4,32,96,256]{3,2,0,1:T(8,128)(2,1)} fusion(bf16[4,32,96,256]{3,2,0,1:T(8,128)(2,1)} %get-tuple-element.794, s32[]{:T(128)S(6)} %select_n.114, bf16[32,4,256,256]{3,2,1,0:T(8,128)(2,1)} %get-tuple-element.808, bf16[4,32,160,256]{3,2,0,1:T(8,128)(2,1)} %get-tuple-element.809, f32[4,96,256]{2,1,0:T(8,128)S(1)} %broadcast_multiply_fusion.11, ...), kind=kOutput, calls=%fused_computation.11.clone.1 | convolution fusion | flops 1311768576 | bytes 5867520 | tf_op jit(solution)/shard_map/while/body/eval_jaxpr/kswic,wkcd->swid/dot_general | solution.py:173
  177.0 5.5 %fusion.115 = (bf16[4,32,32,256]{3,2,0,1:T(8,128)(2,1)}, bf16[4,32,32,256]{3,2,0,1:T(8,128)(2,1)}) fusion(bf16[4,32,96,256]{3,2,0,1:T(8,128)(2,1)} %get-tuple-element.364, s32[]{:T(128)S(6)} %select_n.92), kind=kLoop, calls=%fused_computation.221 | loop fusion | bytes 8388612 | tf_op jit(solution)/shard_map/slice | solution.py:188
  184.3 5.4 %collective-permute-start.6 = (bf16[4,32,32,256]{3,2,0,1:T(8,128)(2,1)}, bf16[4,32,32,256]{3,2,0,1:T(8,128)(2,1)}, u32[]{:S(2)}, u32[]{:S(2)}) collective-permute-start(bf16[4,32,32,256]{3,2,0,1:T(8,128)(2,1)} %get-tuple-element.555), channel_id=1, source_target_pairs={{1,0},{2,1},{3,2},{4,3},{5,4},{6,5},{7,6},{8,7},{9,8},{10,9},{11,1... | collective-permute-start | bytes 6291464 | tf_op jit(solution)/shard_map/ppermute | solution.py:15
  193.9 39.8 %collective-permute-done.5 = bf16[4,32,32,256]{3,2,0,1:T(8,128)(2,1)} collective-permute-done((bf16[4,32,32,256]{3,2,0,1:T(8,128)(2,1)}, bf16[4,32,32,256]{3,2,0,1:T(8,128)(2,1)}, u32[]{:S(2)}, u32[]{:S(2)}) %collective-permute-start.5) | collective-permute-done | bytes 2097184 | tf_op jit(solution)/shard_map/ppermute | solution.py:15
  233.7 10.1 %maximum_maximum_fusion.1 = bf16[4,32,160,256]{3,2,0,1:T(8,128)(2,1)} fusion(bf16[4,32,96,256]{3,2,0,1:T(8,128)(2,1)} %get-tuple-element.364, bf16[4,32,32,256]{3,2,0,1:T(8,128)(2,1)} %collective-permute-done.5, bf16[160]{0:T(256)(128)(2,1)S(1)} %pad.113.clone), kind=kLoop, calls=%fused_computation.153 | loop fusion | flops 31457280 | bytes 18874688 | tf_op jit(solution)/shard_map/concatenate | solution.py:130
  243.8 20.4 %dynamic_update_slice.14 = bf16[4,32,160,256]{3,2,0,1:T(8,128)(2,1)} dynamic-update-slice(bf16[4,32,160,256]{3,2,0,1:T(8,128)(2,1)} %maximum_maximum_fusion.1, bf16[4,32,32,256]{3,2,0,1:T(8,128)(2,1)} %collective-permute-done.6, s32[]{:T(128)} %constant.285.clone.1, s32[]{:T(128)} %constant.285.clone.1, s32[]{:T(128)S(6)} %select_n.93, s32[]{:T(128)} %constant.285.clone.1) | dynamic-update-slice | bytes 4194308 | tf_op jit(solution)/shard_map/dynamic_update_slice | solution.py:131
  264.2 134.8 %while.32 = (s32[]{:T(128)}, f32[9,96,256]{2,1,0:T(8,128)S(1)}, f32[9,96,256]{2,1,0:T(8,128)S(1)}, f32[32]{0:T(128)S(1)}, bf16[32,4,256,256]{3,2,1,0:T(8,128)(2,...) while((s32[]{:T(128)}, f32[9,96,256]{2,1,0:T(8,128)S(1)}, ...), condition=%wide.region_21.22_spmd.clone, body=%wide.region_2.21_spmd.clone.sunk | while | flops 1872642304 | bytes 34342920 | solution.py:211
  284.2 4.9 %fusion.137 = f32[4,4,96,256]{3,2,0,1:T(8,128)S(1)} fusion(bf16[32,4,256,256]{3,2,1,0:T(8,128)(2,1)} %get-tuple-element.845, s32[]{:T(128)S(6)} %select_n.115, bf16[4,32,160,256]{3,2,0,1:T(8,128)(2,1)} %get-tuple-element.846, f32[96]{0:T(128)S(1)} %compare_convert_fusion.3, bf16[4,4,96,160]{2,0,1,3:T(4,128)(2,1)} %constant_dynamic-slice_fusion.13), kind=kOutput, calls=%fused_computation.27.clone.1 | convolution fusion | flops 1848508416 | bytes 5637504 | tf_op jit(solution)/shard_map/while/body/eval_jaxpr/wkij,kswjc->swic/dot_general | solution.py:201
  301.1 4.9 %fusion.137 = f32[4,4,96,256]{3,2,0,1:T(8,128)S(1)} fusion(bf16[32,4,256,256]{3,2,1,0:T(8,128)(2,1)} %get-tuple-element.845, s32[]{:T(128)S(6)} %select_n.115, bf16[4,32,160,256]{3,2,0,1:T(8,128)(2,1)} %get-tuple-element.846, f32[96]{0:T(128)S(1)} %compare_convert_fusion.3, bf16[4,4,96,160]{2,0,1,3:T(4,128)(2,1)} %constant_dynamic-slice_fusion.13), kind=kOutput, calls=%fused_computation.27.clone.1 | convolution fusion | flops 1848508416 | bytes 5637504 | tf_op jit(solution)/shard_map/while/body/eval_jaxpr/wkij,kswjc->swic/dot_general | solution.py:201
  317.9 4.9 %fusion.137 = f32[4,4,96,256]{3,2,0,1:T(8,128)S(1)} fusion(bf16[32,4,256,256]{3,2,1,0:T(8,128)(2,1)} %get-tuple-element.845, s32[]{:T(128)S(6)} %select_n.115, bf16[4,32,160,256]{3,2,0,1:T(8,128)(2,1)} %get-tuple-element.846, f32[96]{0:T(128)S(1)} %compare_convert_fusion.3, bf16[4,4,96,160]{2,0,1,3:T(4,128)(2,1)} %constant_dynamic-slice_fusion.13), kind=kOutput, calls=%fused_computation.27.clone.1 | convolution fusion | flops 1848508416 | bytes 5637504 | tf_op jit(solution)/shard_map/while/body/eval_jaxpr/wkij,kswjc->swic/dot_general | solution.py:201
  334.8 4.9 %fusion.137 = f32[4,4,96,256]{3,2,0,1:T(8,128)S(1)} fusion(bf16[32,4,256,256]{3,2,1,0:T(8,128)(2,1)} %get-tuple-element.845, s32[]{:T(128)S(6)} %select_n.115, bf16[4,32,160,256]{3,2,0,1:T(8,128)(2,1)} %get-tuple-element.846, f32[96]{0:T(128)S(1)} %compare_convert_fusion.3, bf16[4,4,96,160]{2,0,1,3:T(4,128)(2,1)} %constant_dynamic-slice_fusion.13), kind=kOutput, calls=%fused_computation.27.clone.1 | convolution fusion | flops 1848508416 | bytes 5637504 | tf_op jit(solution)/shard_map/while/body/eval_jaxpr/wkij,kswjc->swic/dot_general | solution.py:201
  351.6 4.9 %fusion.137 = f32[4,4,96,256]{3,2,0,1:T(8,128)S(1)} fusion(bf16[32,4,256,256]{3,2,1,0:T(8,128)(2,1)} %get-tuple-element.845, s32[]{:T(128)S(6)} %select_n.115, bf16[4,32,160,256]{3,2,0,1:T(8,128)(2,1)} %get-tuple-element.846, f32[96]{0:T(128)S(1)} %compare_convert_fusion.3, bf16[4,4,96,160]{2,0,1,3:T(4,128)(2,1)} %constant_dynamic-slice_fusion.13), kind=kOutput, calls=%fused_computation.27.clone.1 | convolution fusion | flops 1848508416 | bytes 5637504 | tf_op jit(solution)/shard_map/while/body/eval_jaxpr/wkij,kswjc->swic/dot_general | solution.py:201
  368.5 4.9 %fusion.137 = f32[4,4,96,256]{3,2,0,1:T(8,128)S(1)} fusion(bf16[32,4,256,256]{3,2,1,0:T(8,128)(2,1)} %get-tuple-element.845, s32[]{:T(128)S(6)} %select_n.115, bf16[4,32,160,256]{3,2,0,1:T(8,128)(2,1)} %get-tuple-element.846, f32[96]{0:T(128)S(1)} %compare_convert_fusion.3, bf16[4,4,96,160]{2,0,1,3:T(4,128)(2,1)} %constant_dynamic-slice_fusion.13), kind=kOutput, calls=%fused_computation.27.clone.1 | convolution fusion | flops 1848508416 | bytes 5637504 | tf_op jit(solution)/shard_map/while/body/eval_jaxpr/wkij,kswjc->swic/dot_general | solution.py:201
  385.4 4.9 %fusion.137 = f32[4,4,96,256]{3,2,0,1:T(8,128)S(1)} fusion(bf16[32,4,256,256]{3,2,1,0:T(8,128)(2,1)} %get-tuple-element.845, s32[]{:T(128)S(6)} %select_n.115, bf16[4,32,160,256]{3,2,0,1:T(8,128)(2,1)} %get-tuple-element.846, f32[96]{0:T(128)S(1)} %compare_convert_fusion.3, bf16[4,4,96,160]{2,0,1,3:T(4,128)(2,1)} %constant_dynamic-slice_fusion.13), kind=kOutput, calls=%fused_computation.27.clone.1 | convolution fusion | flops 1848508416 | bytes 5637504 | tf_op jit(solution)/shard_map/while/body/eval_jaxpr/wkij,kswjc->swic/dot_general | solution.py:201
  401.1 6.7 %collective-permute-done.7 = f32[4,9,12,256]{3,0,2,1:T(4,128)S(1)} collective-permute-done((f32[4,9,12,256]{3,0,2,1:T(4,128)S(1)}, f32[4,9,12,256]{3,0,2,1:T(4,128)S(1)}, u32[]{:S(2)}, u32[]{:S(2)}) %collective-permute-start.7) | collective-permute-done | bytes 442400 | tf_op jit(solution)/shard_map/ppermute | solution.py:21
  409.5 6.9 %collective-permute-done.8 = f32[2,9,12,256]{3,2,0,1:T(8,128)S(1)} collective-permute-done((f32[2,9,12,256]{3,2,0,1:T(8,128)S(1)}, f32[2,9,12,256]{3,2,0,1:T(8,128)S(1)}, u32[]{:S(2)}, u32[]{:S(2)}) %collective-permute-start.8) | collective-permute-done | bytes 221216 | tf_op jit(solution)/shard_map/ppermute | solution.py:21
  (215 shorter events, 164.2 us)
Async XLA Ops:
  0.0 5.0 %collective-permute-start = (f32[1,27648]{1,0:T(1,128)}, f32[1,27648]{1,0:T(1,128)S(1)}, u32[]{:S(2)}, u32[]{:S(2)}) collective-permute-start(f32[1,27648]{1,0:T(1,128)} %bitcast.280), channel_id=1, source_target_pairs={{0,16},{16,0},{32,48},{48,32},{64,80},{80,64},{96,112},{112,96},{1... | collective-permute-start | bytes 331784 | tf_op jit(solution)/shard_map/ppermute | solution.py:21
  6.3 7.9 %collective-permute-start.1 = (f32[2,27648]{1,0:T(2,128)S(1)}, f32[2,27648]{1,0:T(2,128)S(1)}, u32[]{:S(2)}, u32[]{:S(2)}) collective-permute-start(f32[2,27648]{1,0:T(2,128)S(1)} %maximum_select_fusion.4), channel_id=1, source_target_pairs={{0,32},{16,48},{32,0},{48,16},{64,96},{80,112},{96,64},{112,80},{1... | collective-permute-start | bytes 663560 | tf_op jit(solution)/shard_map/ppermute | solution.py:21
  14.5 10.3 %collective-permute-start.2 = (f32[4,27648]{1,0:T(4,128)S(1)}, f32[4,27648]{1,0:T(4,128)S(1)}, u32[]{:S(2)}, u32[]{:S(2)}) collective-permute-start(f32[4,27648]{1,0:T(4,128)S(1)} %maximum_select_fusion.2), channel_id=1, source_target_pairs={{0,64},{16,80},{32,96},{48,112},{64,0},{80,16},{96,32},{112,48},{1... | collective-permute-start | bytes 1327112 | tf_op jit(solution)/shard_map/ppermute | solution.py:21
  34.0 3.9 copy-start
  34.0 11.2 %copy-start.3 = (bf16[32,4,65]{2,1,0:T(4,128)(2,1)S(1)}, bf16[32,4,65]{2,1,0:T(4,128)(2,1)}, u32[]{:S(2)}) copy-start(bf16[32,4,65]{2,1,0:T(4,128)(2,1)} %param.14) | copy-start | bytes 49924
  37.9 51.6 %collective-permute-start.3 = (bf16[4,32,32,256]{3,2,0,1:T(8,128)(2,1)}, bf16[4,32,32,256]{3,2,0,1:T(8,128)(2,1)}, u32[]{:S(2)}, u32[]{:S(2)}) collective-permute-start(bf16[4,32,32,256]{3,2,0,1:T(8,128)(2,1)} %get-tuple-element.558), channel_id=1, source_target_pairs={{0,1},{1,2},{2,3},{3,4},{4,5},{5,6},{6,7},{7,8},{8,9},{9,10},{10,1... | collective-permute-start | bytes 6291464 | tf_op jit(solution)/shard_map/ppermute | solution.py:15
  39.9 59.8 %collective-permute-start.4 = (bf16[4,32,32,256]{3,2,0,1:T(8,128)(2,1)}, bf16[4,32,32,256]{3,2,0,1:T(8,128)(2,1)}, u32[]{:S(2)}, u32[]{:S(2)}) collective-permute-start(bf16[4,32,32,256]{3,2,0,1:T(8,128)(2,1)} %get-tuple-element.557), channel_id=1, source_target_pairs={{1,0},{2,1},{3,2},{4,3},{5,4},{6,5},{7,6},{8,7},{9,8},{10,9},{11,1... | collective-permute-start | bytes 6291464 | tf_op jit(solution)/shard_map/ppermute | solution.py:15
  53.7 16.4 %copy-start.2 = (s32[96,256]{1,0:T(8,128)S(1)}, s32[96,256]{1,0:T(8,128)}, u32[]{:S(2)}) copy-start(s32[96,256]{1,0:T(8,128)} %param.15) | copy-start | bytes 294916
  53.7 16.4 %copy-start.1 = (bf16[32,4,65]{2,1,0:T(4,128)(2,1)S(1)}, bf16[32,4,65]{2,1,0:T(4,128)(2,1)}, u32[]{:S(2)}) copy-start(bf16[32,4,65]{2,1,0:T(4,128)(2,1)} %param.13) | copy-start | bytes 49924
  120.1 3.4 copy-start.4
  182.4 51.3 %collective-permute-start.5 = (bf16[4,32,32,256]{3,2,0,1:T(8,128)(2,1)}, bf16[4,32,32,256]{3,2,0,1:T(8,128)(2,1)}, u32[]{:S(2)}, u32[]{:S(2)}) collective-permute-start(bf16[4,32,32,256]{3,2,0,1:T(8,128)(2,1)} %get-tuple-element.556), channel_id=1, source_target_pairs={{0,1},{1,2},{2,3},{3,4},{4,5},{5,6},{6,7},{7,8},{8,9},{9,10},{10,1... | collective-permute-start | bytes 6291464 | tf_op jit(solution)/shard_map/ppermute | solution.py:15
  184.3 59.5 %collective-permute-start.6 = (bf16[4,32,32,256]{3,2,0,1:T(8,128)(2,1)}, bf16[4,32,32,256]{3,2,0,1:T(8,128)(2,1)}, u32[]{:S(2)}, u32[]{:S(2)}) collective-permute-start(bf16[4,32,32,256]{3,2,0,1:T(8,128)(2,1)} %get-tuple-element.555), channel_id=1, source_target_pairs={{1,0},{2,1},{3,2},{4,3},{5,4},{6,5},{7,6},{8,7},{9,8},{10,9},{11,1... | collective-permute-start | bytes 6291464 | tf_op jit(solution)/shard_map/ppermute | solution.py:15
  399.5 8.4 %collective-permute-start.7 = (f32[4,9,12,256]{3,0,2,1:T(4,128)S(1)}, f32[4,9,12,256]{3,0,2,1:T(4,128)S(1)}, u32[]{:S(2)}, u32[]{:S(2)}) collective-permute-start(f32[4,9,12,256]{3,0,2,1:T(4,128)S(1)} %copy.63), channel_id=1, source_target_pairs={{0,64},{16,80},{32,96},{48,112},{64,0},{80,16},{96,32},{112,48},{1... | collective-permute-start | bytes 1327112 | tf_op jit(solution)/shard_map/ppermute | solution.py:21
  408.0 8.3 %collective-permute-start.8 = (f32[2,9,12,256]{3,2,0,1:T(8,128)S(1)}, f32[2,9,12,256]{3,2,0,1:T(8,128)S(1)}, u32[]{:S(2)}, u32[]{:S(2)}) collective-permute-start(f32[2,9,12,256]{3,2,0,1:T(8,128)S(1)} %constant_dynamic-slice_fusion.4), channel_id=1, source_target_pairs={{0,32},{16,48},{32,0},{48,16},{64,96},{80,112},{96,64},{112,80},{1... | collective-permute-start | bytes 663560 | tf_op jit(solution)/shard_map/ppermute | solution.py:21
  416.4 5.2 %collective-permute-start.9 = (f32[1,9,12,256]{3,2,0,1:T(8,128)S(1)}, f32[1,9,12,256]{3,2,0,1:T(8,128)S(1)}, u32[]{:S(2)}, u32[]{:S(2)}) collective-permute-start(f32[1,9,12,256]{3,2,0,1:T(8,128)S(1)} %constant_dynamic-slice_fusion.3), channel_id=1, source_target_pairs={{0,16},{16,0},{32,48},{48,32},{64,80},{80,64},{96,112},{112,96},{1... | collective-permute-start | bytes 331784 | tf_op jit(solution)/shard_map/ppermute | solution.py:21

commit v2 on v1

--- a/solution.py
+++ b/solution.py
@@ -127,8 +127,19 @@
 
 def extend(upper_rim, middle, lower_rim, length, axis_index):
     radius = upper_rim.shape[axis_index]
-    widened = jnp.concatenate([upper_rim, middle, jnp.zeros_like(upper_rim)], axis=axis_index)
-    return lax.dynamic_update_slice_in_dim(widened, lower_rim, radius + length, axis_index)
+    extent = middle.shape[axis_index]
+    wide = extent + 2 * radius
+
+    def padded(part, before, after):
+        widths = [(0, 0)] * part.ndim
+        widths[axis_index] = (before, after)
+        return jnp.pad(part, widths)
+
+    upper_part = padded(upper_rim, 0, wide - radius)
+    middle_part = padded(middle, radius, radius)
+    lower_pool = padded(lower_rim, wide, wide)
+    lower_part = lax.dynamic_slice_in_dim(lower_pool, wide - radius - length, wide, axis_index)
+    return upper_part + middle_part + lower_part
 
 
 def per_device(unit_params, observed, psf_rows, psf_cols, pixel_mask, strip_lengths):
@@ -145,7 +156,7 @@
     length = strip_lengths[0]
     wave_pos = lax.axis_index("wave")
     levels = (wave_pos * wave_count + jnp.arange(wave_count, dtype=jnp.int32)).astype(jnp.float32)
-    wave_grid = -3.0 + 6.0 * levels / (wave_count * lax.axis_size("wave") - 1)
+    wave_grid = -3.0 + 6.0 * levels / (wave_count * wave_total - 1)
     row_index = jnp.arange(capacity, dtype=jnp.int32)
     rows_live = (row_index < length).astype(jnp.float32)
     model_own = (stokes_model(own_params, wave_grid) * rows_live[:, None]).astype(jnp.bfloat16)
@@ -158,59 +169,39 @@
     live_mask = pixel_mask.astype(jnp.float32) * rows_live[:, None]
     weight_square = jnp.array(stokes_weight, jnp.float32)
     weight_square = weight_square * weight_square
-    block_size = 4
-    block_count = wave_count // block_size
-
-    def forward(number, residual_all):
-        first_wave = number * block_size
-        model_block = lax.dynamic_slice_in_dim(model_wide, first_wave, block_size, 1)
-        band_block = lax.dynamic_slice_in_dim(row_band, first_wave, block_size, 0)
-        column_block = lax.dynamic_slice_in_dim(column_band, first_wave, block_size, 0)
-        observed_block = lax.dynamic_slice_in_dim(observed, first_wave, block_size, 1)
-        row_pass = jnp.einsum(
-            "wkij,swjc->kswic", band_block, model_block, preferred_element_type=jnp.float32
-        ).astype(jnp.bfloat16)
-        blurred = jnp.einsum(
-            "kswic,wkcd->swid", row_pass, column_block, preferred_element_type=jnp.float32
-        )
-        residual = (
-            loss_scale
-            * weight_square[:, None, None, None]
-            * live_mask
-            * (blurred - observed_block.astype(jnp.float32))
-        ).astype(jnp.bfloat16)
-        return lax.dynamic_update_slice_in_dim(residual_all, residual, first_wave, 1)
-
-    residual_all = lax.fori_loop(0, block_count, forward, jnp.zeros(observed.shape, jnp.bfloat16))
+
+    row_pass = jnp.einsum(
+        "wkij,swjc->kswic", row_band, model_wide, preferred_element_type=jnp.float32
+    ).astype(jnp.bfloat16)
+    blurred = jnp.einsum(
+        "kswic,wkcd->swid", row_pass, column_band, preferred_element_type=jnp.float32
+    )
+    residual_all = (
+        loss_scale
+        * weight_square[:, None, None, None]
+        * live_mask
+        * (blurred - observed.astype(jnp.float32))
+    ).astype(jnp.bfloat16)
+
     row_back = band_tables(psf_rows[:, :, ::-1], capacity, tap_count)
     tail_residual = lax.dynamic_slice_in_dim(residual_all, length - radius, radius, 2)
     upper_resid = passed_along(tail_residual, "strip", 1)
     lower_resid = passed_along(residual_all[:, :, :radius], "strip", -1)
     residual_wide = extend(upper_resid, residual_all, lower_resid, length, 2)
 
-    def backward(number, gradient_sum):
-        first_wave = number * block_size
-        residual_block = lax.dynamic_slice_in_dim(residual_wide, first_wave, block_size, 1)
-        column_block = lax.dynamic_slice_in_dim(column_band, first_wave, block_size, 0)
-        back_block = lax.dynamic_slice_in_dim(row_back, first_wave, block_size, 0)
-        grid_block = lax.dynamic_slice_in_dim(wave_grid, first_wave, block_size, 0)
-        across = jnp.einsum(
-            "swjc,wkdc->kswjd", residual_block, column_block, preferred_element_type=jnp.float32
-        ).astype(jnp.bfloat16)
-        adjoint = (
-            jnp.einsum("wkij,kswjc->swic", back_block, across, preferred_element_type=jnp.float32)
-            * rows_live[:, None]
-        )
-
-        def model_of(params_now):
-            return stokes_model(params_now, grid_block)
-
-        unused_model, pullback = jax.vjp(model_of, own_params)
-        return gradient_sum + pullback(adjoint)[0]
-
-    gradient_local = lax.fori_loop(
-        0, block_count, backward, jnp.zeros(own_params.shape, jnp.float32)
-    )
+    across = jnp.einsum(
+        "swjc,wkdc->kswjd", residual_wide, column_band, preferred_element_type=jnp.float32
+    ).astype(jnp.bfloat16)
+    adjoint = (
+        jnp.einsum("wkij,kswjc->swic", row_back, across, preferred_element_type=jnp.float32)
+        * rows_live[:, None]
+    )
+
+    def model_of(params_now):
+        return stokes_model(params_now, wave_grid)
+
+    unused_model, pullback = jax.vjp(model_of, own_params)
+    gradient_local = pullback(adjoint)[0]
     pieces = gradient_local.reshape(
         gradient_local.shape[0], wave_total, capacity // wave_total, columns
     ).transpose(1, 0, 2, 3)

time: 426 us -> 349 us (0.82)
  local copies, waits for them, and re-layouts: 107 us -> 17.4 us
  other arithmetic: 108 us -> 48.1 us
  matrix products: 94.7 us -> 154 us
  waiting for transfers between devices: 88.8 us -> 97.8 us
    dot_general x16 -> x2, matrix products: 78.4 us -> 137 us  [the longest x1 83.4 us: per_device(): jnp.einsum('wkij,kswjc->swic', row_back, across, preferred_element_type=j...]
    dynamic_update_slice x2 -> x0, local copies, waits for them, and re-layouts: 40.8 us -> none  [extend(): lax.dynamic_update_slice_in_dim(widened, lower_rim, radius + length, axis...]
    dynamic_slice x24 -> x2, local copies, waits for them, and re-layouts: 34.1 us -> 8.07 us  [the longest x1 4.96 us: per_device(): lax.dynamic_slice_in_dim(residual_all, length - radius, radius, 2)]
    mul x32 -> x8, other arithmetic: 22.7 us -> 0.87 us  [stokes_model(): parameter_span[number] * unit_params[number]]
    concatenate x2 -> x0, other arithmetic: 20.2 us -> none  [extend(): jnp.concatenate([upper_rim, middle, jnp.zeros_like(upper_rim)], axis=axis...]
    unnamed x11 -> x46, local copies, waits for them, and re-layouts: 16.5 us -> 1.04 us
    add x10 -> x1, other arithmetic: 11.5 us -> 0.01 us  [per_device(): wave_grid = -3.0 + 6.0 * levels / (wave_count * wave_total - 1)]
    mul x32 -> x3, other arithmetic: 12.7 us -> 1.53 us  [the longest x1 0.86 us: per_device(): loss_scale * weight_square[:, None, None, None] * live_mask]
  transfers between devices with their start and end apart: 10 -> 10, of which waited for: 8 -> 8; matrix products, arithmetic and copies ran while one was open for 13% -> 8% of each run, Pallas kernels for 0% -> 0%
where the time goes in v2:
time: 349 us; the launch traced here: 342 us
  matrix products  154 us (44%)
  waiting for transfers between devices  97.8 us (28%)
  other arithmetic  48.1 us (14%)
  starting transfers between devices  22.6 us (6%)
  local copies, waits for them, and re-layouts  17.4 us (5%)
    dot_general x1, matrix products, per_device(): jnp.einsum('wkij,kswjc->swic', row_back, across, preferred_element_type=j...  83.4 us
    ppermute x4, waiting for transfers between devices, passed_along(): return lax.ppermute(shard, axis, pairs)  64.5 us
    dot_general x1, matrix products, per_device(): jnp.einsum('kswic,wkcd->swid', row_pass, column_band, preferred_element_t...  53.7 us
    ppermute x6, waiting for transfers between devices, exchange(): return lax.ppermute(shard, axis, pairs)  33.3 us
    add_any x1, other arithmetic, profile(): scaled = distance / damping  14.7 us
    ppermute x4, starting transfers between devices, passed_along(): return lax.ppermute(shard, axis, pairs)  14.5 us
    dot_general x2, matrix products, band_tables(): jnp.einsum('wkt,ijt->wkij', tap_table, selector, preferred_element_type=j...  8.91 us
    dot_general x1, matrix products, column_tables(): jnp.einsum('wkt,xyt->wkxy', tap_table, selector, preferred_element_type=j...  8.39 us
  transfers between devices with their start and end apart: 10, of which 8 were waited for; matrix products, arithmetic and copies ran while one was open for 8% of the time, Pallas kernels for 0%

profile of v2, /device:TPU:78, one launch (start us, length us, event | category | flops | bytes accessed | tf_op | source)
XLA Modules:
  0.0 342.1 jit_solution(7358089081689422244)
XLA Ops:
  0.8 4.2 %collective-permute-done = f32[1,27648]{1,0:T(1,128)S(1)} collective-permute-done((f32[1,27648]{1,0:T(1,128)}, f32[1,27648]{1,0:T(1,128)S(1)}, u32[]{:S(2)}, u32[]{:S(2)}) %collective-permute-start) | collective-permute-done | bytes 110624 | tf_op jit(solution)/shard_map/ppermute | solution.py:21
  6.3 1.5 collective-permute-start.1
  9.7 4.5 %collective-permute-done.1 = f32[2,27648]{1,0:T(2,128)S(1)} collective-permute-done((f32[2,27648]{1,0:T(2,128)S(1)}, f32[2,27648]{1,0:T(2,128)S(1)}, u32[]{:S(2)}, u32[]{:S(2)}) %collective-permute-start.1) | collective-permute-done | bytes 221216 | tf_op jit(solution)/shard_map/ppermute | solution.py:21
  14.5 1.7 collective-permute-start.2
  18.0 6.8 %collective-permute-done.2 = f32[4,27648]{1,0:T(4,128)S(1)} collective-permute-done((f32[4,27648]{1,0:T(4,128)S(1)}, f32[4,27648]{1,0:T(4,128)S(1)}, u32[]{:S(2)}, u32[]{:S(2)}) %collective-permute-start.2) | collective-permute-done | bytes 442400 | tf_op jit(solution)/shard_map/ppermute | solution.py:21
  25.3 1.6 fusion.93
  28.5 5.3 %multiply_add_fusion.1 = (f32[1,32,96,256]{3,2,0,1:T(8,128)S(1)}, f32[1,32,96,256]{3,2,0,1:T(8,128)S(1)}, f32[1,32,96,256]{3,2,0,1:T(8,128)S(1)}, f32[1,32,96,256]{3,2,0,1:T(8,128)S(1)}) fusion(f32[96,256]{1,0:T(8,128)S(1)} %get-tuple-element.71, f32[96,256]{1,0:T(8,128)S(1)} %add.419, f32[96,256]{1,0:T(8,128)S(1)} %get-tuple-element.65, ...), kind=kLoop, calls=%fused_computation.80 | loop fusion | flops 37748736 | bytes 13860992 | tf_op jit(solution)/shard_map/add | solution.py:98
  33.9 2.0 fusion.16
  35.9 3.1 constant_dynamic-slice_fusion.4
  39.2 1.9 collective-permute-start.3
  41.1 5.3 %collective-permute-start.4 = (bf16[4,32,32,256]{3,2,0,1:T(8,128)(2,1)S(1)}, bf16[4,32,32,256]{3,2,0,1:T(8,128)(2,1)}, u32[]{:S(2)}, u32[]{:S(2)}) collective-permute-start(bf16[4,32,32,256]{3,2,0,1:T(8,128)(2,1)S(1)} %get-tuple-element.43), channel_id=1, source_target_pairs={{1,0},{2,1},{3,2},{4,3},{5,4},{6,5},{7,6},{8,7},{9,8},{10,9},{11,1... | collective-permute-start | bytes 6291464 | tf_op jit(solution)/shard_map/ppermute | solution.py:15
  46.5 4.5 %convert_bitcast_fusion.2 = bf16[32,4,96,160,1]{3,0,1,2,4:T(8,128)(2,1)} fusion(bf16[32,4,65]{2,1,0:T(4,128)(2,1)S(1)} %copy-done.19), kind=kOutput, calls=%fused_computation.41 | convolution fusion | flops 259553280 | bytes 3948800 | tf_op jit(solution)/shard_map/wkt,ijt->wkij/dot_general | solution.py:112
  51.9 8.4 %convert_bitcast_fusion = bf16[32,4,256,256,1]{3,0,1,2,4:T(8,128)(2,1)} fusion(bf16[32,4,65]{2,1,0:T(4,128)(2,1)S(1)} %copy-done.22), kind=kOutput, calls=%fused_computation.12 | convolution fusion | flops 1111687168 | bytes 16793856 | tf_op jit(solution)/shard_map/wkt,xyt->wkxy/dot_general | solution.py:123
  60.3 30.5 %collective-permute-done.3 = bf16[4,32,32,256]{3,2,0,1:T(8,128)(2,1)} collective-permute-done((bf16[4,32,32,256]{3,2,0,1:T(8,128)(2,1)}, bf16[4,32,32,256]{3,2,0,1:T(8,128)(2,1)}, u32[]{:S(2)}, u32[]{:S(2)}) %collective-permute-start.3) | collective-permute-done | bytes 2097184 | tf_op jit(solution)/shard_map/ppermute | solution.py:15
  90.8 53.7 %fusion.18 = bf16[4,32,96,256]{3,2,0,1:T(8,128)(2,1)} fusion(bf16[4,32,96,256]{3,2,1,0:T(8,128)(2,1)} %param.8, f32[4,96,256]{2,1,0:T(8,128)} %broadcast_multiply_fusion, s32[]{:T(128)S(6)} %select_n.68, bf16[4,32,32,256]{3,2,0,1:T(8,128)(2,1)} %collective-permute-done.4, bf16[4,32,96,256]{3,2,0,1:T(8,128)(2,1)} %copy-done, ...), kind=kOutput, calls=%fused_computation.20 | convolution fusion | flops 10525605888 | bytes 44171268 | tf_op jit(solution)/shard_map/kswic,wkcd->swid/dot_general | solution.py:176
  144.5 5.0 %constant_dynamic-slice_fusion.3 = (bf16[4,32,32,256]{3,2,0,1:T(8,128)(2,1)}, bf16[4,32,32,256]{3,2,0,1:T(8,128)(2,1)S(1)}) fusion(bf16[4,32,96,256]{3,2,0,1:T(8,128)(2,1)} %fusion.18, s32[]{:T(128)S(6)} %select_n.67), kind=kLoop, calls=%fused_computation.184 | loop fusion | bytes 8388612 | tf_op jit(solution)/shard_map/dynamic_slice | solution.py:187
  149.5 2.1 collective-permute-start.5
  151.6 5.1 %collective-permute-start.6 = (bf16[4,32,32,256]{3,2,0,1:T(8,128)(2,1)S(1)}, bf16[4,32,32,256]{3,2,0,1:T(8,128)(2,1)}, u32[]{:S(2)}, u32[]{:S(2)}) collective-permute-start(bf16[4,32,32,256]{3,2,0,1:T(8,128)(2,1)S(1)} %get-tuple-element.41), channel_id=1, source_target_pairs={{1,0},{2,1},{3,2},{4,3},{5,4},{6,5},{7,6},{8,7},{9,8},{10,9},{11,1... | collective-permute-start | bytes 6291464 | tf_op jit(solution)/shard_map/ppermute | solution.py:15
  156.9 4.4 %convert_bitcast_fusion.1 = bf16[32,4,96,160,1]{3,0,1,2,4:T(8,128)(2,1)} fusion(bf16[32,4,65]{2,1,0:T(4,128)(2,1)S(1)} %rev.3), kind=kOutput, calls=%fused_computation.40 | convolution fusion | flops 259553280 | bytes 3948800 | tf_op jit(solution)/shard_map/wkt,ijt->wkij/dot_general | solution.py:112
  165.0 1.7 sin.44
  167.3 34.0 %collective-permute-done.5 = bf16[4,32,32,256]{3,2,0,1:T(8,128)(2,1)} collective-permute-done((bf16[4,32,32,256]{3,2,0,1:T(8,128)(2,1)}, bf16[4,32,32,256]{3,2,0,1:T(8,128)(2,1)}, u32[]{:S(2)}, u32[]{:S(2)}) %collective-permute-start.5) | collective-permute-done | bytes 2097184 | tf_op jit(solution)/shard_map/ppermute | solution.py:15
  201.3 83.4 %fusion.19 = f32[4,32,96,256]{3,2,0,1:T(8,128)} fusion(f32[96]{0:T(128)S(1)} %compare_convert_fusion, bf16[32,4,256,256,1]{3,0,1,2,4:T(8,128)(2,1)} %convert_bitcast_fusion, s32[]{:T(128)S(6)} %select_n.68, bf16[4,32,32,256]{3,2,0,1:T(8,128)(2,1)} %collective-permute-done.6, bf16[4,32,96,256]{3,2,0,1:T(8,128)(2,1)} %fusion.18, ...), kind=kOutput, calls=%fused_computation.22 | convolution fusion | flops 14819524608 | bytes 43778436 | tf_op jit(solution)/shard_map/wkij,kswjc->swic/dot_general | solution.py:196
  284.8 2.7 slice_reduce_fusion
  287.5 14.7 %divide_add_fusion = (f32[32,96,256]{2,1,0:T(8,128)S(1)}, f32[32,96,256]{2,1,0:T(8,128)S(1)}, f32[32,96,256]{2,1,0:T(8,128)S(1)}, f32[32,96,256]{2,1,0:T(8,128)S...) fusion(f32[96,256]{1,0:T(8,128)S(1)} %add.419, ...), kind=kLoop, calls=%fused_computation.67 | loop fusion | flops 90439680 | bytes 45711488 | tf_op jit(solution)/shard_map/transpose(jvp())/add_any | solution.py:55
  302.3 8.2 %multiply_reduce_fusion.6 = (f32[96,256]{1,0:T(8,128)S(1)}, f32[96,256]{1,0:T(8,128)S(1)}, f32[96,256]{1,0:T(8,128)S(1)}, f32[96,256]{1,0:T(8,128)S(1)}, f32[96,...) fusion(f32[32,96,256]{2,1,0:T(8,128)S(1)} %get-tuple-element.38, ...), kind=kLoop, calls=%fused_computation.72 | loop fusion | flops 49348608 | bytes 17694848 | tf_op jit(solution)/shard_map/transpose(jvp())/reduce_sum | solution.py:83
  310.5 4.5 %multiply_reduce_fusion.4 = (f32[96,256]{1,0:T(8,128)S(1)}, f32[96,256]{1,0:T(8,128)S(1)}, f32[96,256]{1,0:T(8,128)S(1)}, f32[96,256]{1,0:T(8,128)S(1)}, f32[96,...) fusion(f32[32,96,256]{2,1,0:T(8,128)S(1)} %get-tuple-element.33, ...), kind=kLoop, calls=%fused_computation.69 | loop fusion | flops 29663232 | bytes 17399936 | tf_op jit(solution)/shard_map/transpose(jvp())/reduce_sum | solution.py:55
  316.8 1.3 pad_add_fusion
  318.6 1.7 collective-permute-start.7
  320.3 6.7 %collective-permute-done.7 = f32[4,9,12,256]{3,0,2,1:T(4,128)S(1)} collective-permute-done((f32[4,9,12,256]{3,0,2,1:T(4,128)S(1)}, f32[4,9,12,256]{3,0,2,1:T(4,128)S(1)}, u32[]{:S(2)}, u32[]{:S(2)}) %collective-permute-start.7) | collective-permute-done | bytes 442400 | tf_op jit(solution)/shard_map/ppermute | solution.py:21
  327.3 1.5 collective-permute-start.8
  328.8 6.8 %collective-permute-done.8 = f32[2,9,12,256]{3,2,0,1:T(8,128)S(1)} collective-permute-done((f32[2,9,12,256]{3,2,0,1:T(8,128)S(1)}, f32[2,9,12,256]{3,2,0,1:T(8,128)S(1)}, u32[]{:S(2)}, u32[]{:S(2)}) %collective-permute-start.8) | collective-permute-done | bytes 221216 | tf_op jit(solution)/shard_map/ppermute | solution.py:21
  336.6 4.3 %collective-permute-done.9 = f32[1,9,12,256]{3,2,0,1:T(8,128)S(1)} collective-permute-done((f32[1,9,12,256]{3,2,0,1:T(8,128)S(1)}, f32[1,9,12,256]{3,2,0,1:T(8,128)S(1)}, u32[]{:S(2)}, u32[]{:S(2)}) %collective-permute-start.9) | collective-permute-done | bytes 110624 | tf_op jit(solution)/shard_map/ppermute | solution.py:21
  (111 shorter events, 17.1 us)
Async XLA Ops:
  0.0 5.0 %collective-permute-start = (f32[1,27648]{1,0:T(1,128)}, f32[1,27648]{1,0:T(1,128)S(1)}, u32[]{:S(2)}, u32[]{:S(2)}) collective-permute-start(f32[1,27648]{1,0:T(1,128)} %bitcast.143), channel_id=1, source_target_pairs={{0,16},{16,0},{32,48},{48,32},{64,80},{80,64},{96,112},{112,96},{1... | collective-permute-start | bytes 331784 | tf_op jit(solution)/shard_map/ppermute | solution.py:21
  6.3 7.9 %collective-permute-start.1 = (f32[2,27648]{1,0:T(2,128)S(1)}, f32[2,27648]{1,0:T(2,128)S(1)}, u32[]{:S(2)}, u32[]{:S(2)}) collective-permute-start(f32[2,27648]{1,0:T(2,128)S(1)} %maximum_select_fusion.4), channel_id=1, source_target_pairs={{0,32},{16,48},{32,0},{48,16},{64,96},{80,112},{96,64},{112,80},{1... | collective-permute-start | bytes 663560 | tf_op jit(solution)/shard_map/ppermute | solution.py:21
  14.5 10.3 %collective-permute-start.2 = (f32[4,27648]{1,0:T(4,128)S(1)}, f32[4,27648]{1,0:T(4,128)S(1)}, u32[]{:S(2)}, u32[]{:S(2)}) collective-permute-start(f32[4,27648]{1,0:T(4,128)S(1)} %maximum_select_fusion.2), channel_id=1, source_target_pairs={{0,64},{16,80},{32,96},{48,112},{64,0},{80,16},{96,32},{112,48},{1... | collective-permute-start | bytes 1327112 | tf_op jit(solution)/shard_map/ppermute | solution.py:21
  27.1 0.6 copy-start.9
  27.1 139.6 %copy-start.1 = (f32[96,256]{1,0:T(8,128)}, f32[96,256]{1,0:T(8,128)S(1)}, u32[]{:S(2)}) copy-start(f32[96,256]{1,0:T(8,128)S(1)} %mul.1336) | copy-start | bytes 294916
  27.2 6.7 %copy-start.7 = (f32[96,256]{1,0:T(8,128)}, f32[96,256]{1,0:T(8,128)S(1)}, u32[]{:S(2)}) copy-start(f32[96,256]{1,0:T(8,128)S(1)} %add.426) | copy-start | bytes 294916
  27.7 6.1 %copy-start.4 = (f32[96,256]{1,0:T(8,128)}, f32[96,256]{1,0:T(8,128)S(1)}, u32[]{:S(2)}) copy-start(f32[96,256]{1,0:T(8,128)S(1)} %get-tuple-element.74) | copy-start | bytes 294916
  27.7 6.1 %copy-start.5 = (f32[96,256]{1,0:T(8,128)}, f32[96,256]{1,0:T(8,128)S(1)}, u32[]{:S(2)}) copy-start(f32[96,256]{1,0:T(8,128)S(1)} %get-tuple-element.75) | copy-start | bytes 294916
  28.5 5.3 %copy-start.2 = (f32[96,256]{1,0:T(8,128)}, f32[96,256]{1,0:T(8,128)S(1)}, u32[]{:S(2)}) copy-start(f32[96,256]{1,0:T(8,128)S(1)} %get-tuple-element.66) | copy-start | bytes 294916
  28.5 5.3 %copy-start.3 = (f32[96,256]{1,0:T(8,128)}, f32[96,256]{1,0:T(8,128)S(1)}, u32[]{:S(2)}) copy-start(f32[96,256]{1,0:T(8,128)S(1)} %get-tuple-element.71) | copy-start | bytes 294916
  35.9 3.3 copy-start
  35.9 10.5 %copy-start.19 = (bf16[32,4,65]{2,1,0:T(4,128)(2,1)S(1)}, bf16[32,4,65]{2,1,0:T(4,128)(2,1)}, u32[]{:S(2)}) copy-start(bf16[32,4,65]{2,1,0:T(4,128)(2,1)} %param.9) | copy-start | bytes 49924
  39.2 51.6 %collective-permute-start.3 = (bf16[4,32,32,256]{3,2,0,1:T(8,128)(2,1)}, bf16[4,32,32,256]{3,2,0,1:T(8,128)(2,1)}, u32[]{:S(2)}, u32[]{:S(2)}) collective-permute-start(bf16[4,32,32,256]{3,2,0,1:T(8,128)(2,1)} %get-tuple-element.42), channel_id=1, source_target_pairs={{0,1},{1,2},{2,3},{3,4},{4,5},{5,6},{6,7},{7,8},{8,9},{9,10},{10,1... | collective-permute-start | bytes 6291464 | tf_op jit(solution)/shard_map/ppermute | solution.py:15
  41.1 49.7 %collective-permute-start.4 = (bf16[4,32,32,256]{3,2,0,1:T(8,128)(2,1)S(1)}, bf16[4,32,32,256]{3,2,0,1:T(8,128)(2,1)}, u32[]{:S(2)}, u32[]{:S(2)}) collective-permute-start(bf16[4,32,32,256]{3,2,0,1:T(8,128)(2,1)S(1)} %get-tuple-element.43), channel_id=1, source_target_pairs={{1,0},{2,1},{3,2},{4,3},{5,4},{6,5},{7,6},{8,7},{9,8},{10,9},{11,1... | collective-permute-start | bytes 6291464 | tf_op jit(solution)/shard_map/ppermute | solution.py:15
  46.5 4.5 %copy-start.20 = (s32[96,256]{1,0:T(8,128)S(1)}, s32[96,256]{1,0:T(8,128)}, u32[]{:S(2)}) copy-start(s32[96,256]{1,0:T(8,128)} %param.11) | copy-start | bytes 294916
  46.5 4.6 %copy-start.21 = (f32[4]{0:T(128)S(1)}, f32[4]{0:T(128)}, u32[]{:S(2)}) copy-start(f32[4]{0:T(128)} %constant.119) | copy-start | bytes 52
  46.5 5.5 %copy-start.22 = (bf16[32,4,65]{2,1,0:T(4,128)(2,1)S(1)}, bf16[32,4,65]{2,1,0:T(4,128)(2,1)}, u32[]{:S(2)}) copy-start(bf16[32,4,65]{2,1,0:T(4,128)(2,1)} %param.10) | copy-start | bytes 49924
  149.5 51.8 %collective-permute-start.5 = (bf16[4,32,32,256]{3,2,0,1:T(8,128)(2,1)}, bf16[4,32,32,256]{3,2,0,1:T(8,128)(2,1)}, u32[]{:S(2)}, u32[]{:S(2)}) collective-permute-start(bf16[4,32,32,256]{3,2,0,1:T(8,128)(2,1)} %get-tuple-element.40), channel_id=1, source_target_pairs={{0,1},{1,2},{2,3},{3,4},{4,5},{5,6},{6,7},{7,8},{8,9},{9,10},{10,1... | collective-permute-start | bytes 6291464 | tf_op jit(solution)/shard_map/ppermute | solution.py:15
  151.6 49.7 %collective-permute-start.6 = (bf16[4,32,32,256]{3,2,0,1:T(8,128)(2,1)S(1)}, bf16[4,32,32,256]{3,2,0,1:T(8,128)(2,1)}, u32[]{:S(2)}, u32[]{:S(2)}) collective-permute-start(bf16[4,32,32,256]{3,2,0,1:T(8,128)(2,1)S(1)} %get-tuple-element.41), channel_id=1, source_target_pairs={{1,0},{2,1},{3,2},{4,3},{5,4},{6,5},{7,6},{8,7},{9,8},{10,9},{11,1... | collective-permute-start | bytes 6291464 | tf_op jit(solution)/shard_map/ppermute | solution.py:15
  302.2 8.3 %copy-start.6 = (f32[96,256]{1,0:T(8,128)S(1)}, f32[96,256]{1,0:T(8,128)}, u32[]{:S(2)}) copy-start(f32[96,256]{1,0:T(8,128)} %get-tuple-element.73) | copy-start | bytes 294916
  302.2 8.3 %copy-start.10 = (f32[96,256]{1,0:T(8,128)S(1)}, f32[96,256]{1,0:T(8,128)}, u32[]{:S(2)}) copy-start(f32[96,256]{1,0:T(8,128)} %get-tuple-element.64) | copy-start | bytes 294916
  302.2 8.3 %copy-start.11 = (f32[96,256]{1,0:T(8,128)S(1)}, f32[96,256]{1,0:T(8,128)}, u32[]{:S(2)}) copy-start(f32[96,256]{1,0:T(8,128)} %get-tuple-element.67) | copy-start | bytes 294916
  310.5 5.0 %copy-start.12 = (f32[96,256]{1,0:T(8,128)S(1)}, f32[96,256]{1,0:T(8,128)}, u32[]{:S(2)}) copy-start(f32[96,256]{1,0:T(8,128)} %slice_reduce_fusion) | copy-start | bytes 294916
  315.0 0.9 copy-start.17
  315.0 0.9 copy-start.18
  315.0 1.1 copy-start.15
  315.0 1.1 copy-start.16
  315.0 1.4 copy-start.13
  315.0 1.4 copy-start.14
  318.6 8.4 %collective-permute-start.7 = (f32[4,9,12,256]{3,0,2,1:T(4,128)S(1)}, f32[4,9,12,256]{3,0,2,1:T(4,128)S(1)}, u32[]{:S(2)}, u32[]{:S(2)}) collective-permute-start(f32[4,9,12,256]{3,0,2,1:T(4,128)S(1)} %copy.45), channel_id=1, source_target_pairs={{0,64},{16,80},{32,96},{48,112},{64,0},{80,16},{96,32},{112,48},{1... | collective-permute-start | bytes 1327112 | tf_op jit(solution)/shard_map/ppermute | solution.py:21
  327.3 8.3 %collective-permute-start.8 = (f32[2,9,12,256]{3,2,0,1:T(8,128)S(1)}, f32[2,9,12,256]{3,2,0,1:T(8,128)S(1)}, u32[]{:S(2)}, u32[]{:S(2)}) collective-permute-start(f32[2,9,12,256]{3,2,0,1:T(8,128)S(1)} %constant_dynamic-slice_fusion.1), channel_id=1, source_target_pairs={{0,32},{16,48},{32,0},{48,16},{64,96},{80,112},{96,64},{112,80},{1... | collective-permute-start | bytes 663560 | tf_op jit(solution)/shard_map/ppermute | solution.py:21
  335.7 5.2 %collective-permute-start.9 = (f32[1,9,12,256]{3,2,0,1:T(8,128)S(1)}, f32[1,9,12,256]{3,2,0,1:T(8,128)S(1)}, u32[]{:S(2)}, u32[]{:S(2)}) collective-permute-start(f32[1,9,12,256]{3,2,0,1:T(8,128)S(1)} %constant_dynamic-slice_fusion), channel_id=1, source_target_pairs={{0,16},{16,0},{32,48},{48,32},{64,80},{80,64},{96,112},{112,96},{1... | collective-permute-start | bytes 331784 | tf_op jit(solution)/shard_map/ppermute | solution.py:21
  (1 other events, 0.6 us)

commit v3 on v2

--- a/solution.py
+++ b/solution.py
@@ -56,7 +56,7 @@
     return 1.0 / (1.0 + scaled * scaled)
 
 
-def stokes_model(unit_params, wave_grid):
+def stokes_model(unit_params, wave_grid, stack_axis=0):
     physical = [
         parameter_low[number] + parameter_span[number] * unit_params[number] for number in range(9)
     ]
@@ -99,7 +99,8 @@
             -source_ratio * linear_cosine,
             -source_ratio * linear_sine,
             -source_ratio * circular,
-        ]
+        ],
+        axis=stack_axis,
     )
 
 
@@ -110,7 +111,7 @@
     tap_index = lax.broadcasted_iota(jnp.int32, (out_rows, in_rows, tap_count), 2)
     selector = (source_row - target_row == tap_index).astype(jnp.bfloat16)
     return jnp.einsum(
-        "wkt,ijt->wkij", tap_table, selector, preferred_element_type=jnp.float32
+        "wkt,ijt->kwij", tap_table, selector, preferred_element_type=jnp.float32
     ).astype(jnp.bfloat16)
 
 
@@ -121,7 +122,7 @@
     tap_index = lax.broadcasted_iota(jnp.int32, (columns, columns, tap_count), 2)
     selector = (source_column - target_column + radius == tap_index).astype(jnp.bfloat16)
     return jnp.einsum(
-        "wkt,xyt->wkxy", tap_table, selector, preferred_element_type=jnp.float32
+        "wkt,xyt->kwxy", tap_table, selector, preferred_element_type=jnp.float32
     ).astype(jnp.bfloat16)
 
 
@@ -159,46 +160,65 @@
     wave_grid = -3.0 + 6.0 * levels / (wave_count * wave_total - 1)
     row_index = jnp.arange(capacity, dtype=jnp.int32)
     rows_live = (row_index < length).astype(jnp.float32)
-    model_own = (stokes_model(own_params, wave_grid) * rows_live[:, None]).astype(jnp.bfloat16)
-    tail_rows = lax.dynamic_slice_in_dim(model_own, length - radius, radius, 2)
+    live_rows = rows_live[None, :, None, None]
+    model_own = (stokes_model(own_params, wave_grid, 2) * live_rows).astype(jnp.bfloat16)
+    tail_rows = lax.dynamic_slice_in_dim(model_own, length - radius, radius, 1)
     upper_rim = passed_along(tail_rows, "strip", 1)
-    lower_rim = passed_along(model_own[:, :, :radius], "strip", -1)
-    model_wide = extend(upper_rim, model_own, lower_rim, length, 2)
+    lower_rim = passed_along(model_own[:, :radius], "strip", -1)
+    model_wide = extend(upper_rim, model_own, lower_rim, length, 1)
+    wide_rows = model_wide.shape[1]
     row_band = band_tables(psf_rows, capacity, tap_count)
     column_band = column_tables(psf_cols, columns, tap_count)
     live_mask = pixel_mask.astype(jnp.float32) * rows_live[:, None]
     weight_square = jnp.array(stokes_weight, jnp.float32)
     weight_square = weight_square * weight_square
-
-    row_pass = jnp.einsum(
-        "wkij,swjc->kswic", row_band, model_wide, preferred_element_type=jnp.float32
-    ).astype(jnp.bfloat16)
-    blurred = jnp.einsum(
-        "kswic,wkcd->swid", row_pass, column_band, preferred_element_type=jnp.float32
-    )
+    rank = psf_rows.shape[1]
+
+    model_flat = model_wide.reshape(wave_count, wide_rows, stokes_count * columns)
+    blurred = None
+    for term in range(rank):
+        row_pass = jnp.einsum(
+            "wij,wjn->win", row_band[term], model_flat, preferred_element_type=jnp.float32
+        ).astype(jnp.bfloat16)
+        column_pass = jnp.einsum(
+            "wmc,wcd->wmd",
+            row_pass.reshape(wave_count, capacity * stokes_count, columns),
+            column_band[term],
+            preferred_element_type=jnp.float32,
+        )
+        blurred = column_pass if blurred is None else blurred + column_pass
+    blurred = blurred.reshape(wave_count, capacity, stokes_count, columns)
+    observed_here = observed.transpose(1, 2, 0, 3).astype(jnp.float32)
     residual_all = (
         loss_scale
-        * weight_square[:, None, None, None]
-        * live_mask
-        * (blurred - observed.astype(jnp.float32))
+        * weight_square[None, None, :, None]
+        * live_mask[None, :, None, :]
+        * (blurred - observed_here)
     ).astype(jnp.bfloat16)
 
     row_back = band_tables(psf_rows[:, :, ::-1], capacity, tap_count)
-    tail_residual = lax.dynamic_slice_in_dim(residual_all, length - radius, radius, 2)
+    tail_residual = lax.dynamic_slice_in_dim(residual_all, length - radius, radius, 1)
     upper_resid = passed_along(tail_residual, "strip", 1)
-    lower_resid = passed_along(residual_all[:, :, :radius], "strip", -1)
-    residual_wide = extend(upper_resid, residual_all, lower_resid, length, 2)
-
-    across = jnp.einsum(
-        "swjc,wkdc->kswjd", residual_wide, column_band, preferred_element_type=jnp.float32
-    ).astype(jnp.bfloat16)
-    adjoint = (
-        jnp.einsum("wkij,kswjc->swic", row_back, across, preferred_element_type=jnp.float32)
-        * rows_live[:, None]
-    )
+    lower_resid = passed_along(residual_all[:, :radius], "strip", -1)
+    residual_wide = extend(upper_resid, residual_all, lower_resid, length, 1)
+    residual_flat = residual_wide.reshape(wave_count, wide_rows * stokes_count, columns)
+
+    adjoint = None
+    for term in range(rank):
+        across = jnp.einsum(
+            "wmc,wdc->wmd", residual_flat, column_band[term], preferred_element_type=jnp.float32
+        ).astype(jnp.bfloat16)
+        back_pass = jnp.einsum(
+            "wij,wjn->win",
+            row_back[term],
+            across.reshape(wave_count, wide_rows, stokes_count * columns),
+            preferred_element_type=jnp.float32,
+        )
+        adjoint = back_pass if adjoint is None else adjoint + back_pass
+    adjoint = adjoint.reshape(wave_count, capacity, stokes_count, columns) * live_rows
 
     def model_of(params_now):
-        return stokes_model(params_now, wave_grid)
+        return stokes_model(params_now, wave_grid, 2)
 
     unused_model, pullback = jax.vjp(model_of, own_params)
     gradient_local = pullback(adjoint)[0]

time: 349 us -> 638 us (1.83)
  local copies, waits for them, and re-layouts: 17.4 us -> 192 us
  matrix products: 154 us -> 234 us
  other arithmetic: 48.1 us -> 91.9 us
  waiting for transfers between devices: 97.8 us -> 88.6 us
    reshape x0 -> x10, local copies, waits for them, and re-layouts: none -> 148 us  [the longest x4 68.6 us: per_device(): across.reshape(wave_count, wide_rows, stokes_count * columns)]
    dot_general x5 -> x19, matrix products: 154 us -> 234 us  [the longest x4 85.7 us: per_device(): jnp.einsum('wmc,wdc->wmd', residual_flat, column_band[term], preferred_el...]
    squeeze x0 -> x3, local copies, waits for them, and re-layouts: none -> 17.6 us  [the longest x1 12.5 us: per_device(): column_band[term]]
    mul x1 -> x2, other arithmetic: 0.86 us -> 11.2 us  [the longest x1 11.1 us: per_device(): adjoint.reshape(wave_count, capacity, stokes_count, columns) * live_rows]
    convert_element_type x1 -> x2, other arithmetic: 2.02 us -> 11.6 us  [the longest x1 9.49 us: per_device(): residual_all = (loss_scale * weight_square[None, None, :, None] * live_ma...]
    add x0 -> x1, other arithmetic: none -> 9.09 us  [extend(): return upper_part + middle_part + lower_part]
    unnamed x1 -> x5, other arithmetic: 1.16 us -> 10.2 us
  transfers between devices with their start and end apart: 10 -> 10, of which waited for: 8 -> 7; matrix products, arithmetic and copies ran while one was open for 8% -> 6% of each run, Pallas kernels for 0% -> 0%
where the time goes in v3:
time: 638 us; the launch traced here: 631 us
  matrix products  234 us (37%)
  local copies, waits for them, and re-layouts  192 us (30%)
  other arithmetic  91.9 us (14%)
  waiting for transfers between devices  88.6 us (14%)
  starting transfers between devices  22.2 us (3%)
    dot_general x4, matrix products, per_device(): jnp.einsum('wmc,wdc->wmd', residual_flat, column_band[term], preferred_el...  85.7 us
    reshape x4, local copies, waits for them, and re-layouts, per_device(): across.reshape(wave_count, wide_rows, stokes_count * columns)  68.6 us
    ppermute x4, waiting for transfers between devices, passed_along(): return lax.ppermute(shard, axis, pairs)  58.4 us
    reshape x4, local copies, waits for them, and re-layouts, per_device(): row_pass.reshape(wave_count, capacity * stokes_count, columns)  53.4 us
    dot_general x4, matrix products, per_device(): jnp.einsum('wmc,wcd->wmd', row_pass.reshape(wave_count, capacity * stokes...  53.1 us
    dot_general x4, matrix products, per_device(): jnp.einsum('wij,wjn->win', row_back[term], across.reshape(wave_count, wid...  45.9 us
    dot_general x4, matrix products, per_device(): jnp.einsum('wij,wjn->win', row_band[term], model_flat, preferred_element_...  36.6 us
    ppermute x6, waiting for transfers between devices, exchange(): return lax.ppermute(shard, axis, pairs)  30.2 us
  transfers between devices with their start and end apart: 10, of which 7 were waited for; matrix products, arithmetic and copies ran while one was open for 6% of the time, Pallas kernels for 0%

profile of v3, /device:TPU:78, one launch (start us, length us, event | category | flops | bytes accessed | tf_op | source)
XLA Modules:
  0.0 630.6 jit_solution(3300364918349218662)
XLA Ops:
  74.1 12.5 %slice_bitcast_fusion = (bf16[32,256,256]{2,0,1:T(8,128)(2,1)}, bf16[32,256,256]{2,0,1:T(8,128)(2,1)}, bf16[32,256,256]{2,0,1:T(8,128)(2,1)}, bf16[32,256,256]{2,0,1:T(8,128)(2,1)}) fusion(bf16[4,32,256,256]{3,1,0,2:T(8,128)(2,1)} %convert_bitcast_fusion), kind=kLoop, calls=%fused_computation.41 | loop fusion | bytes 33554432 | tf_op jit(solution)/shard_map/squeeze | solution.py:186
  86.6 23.3 %collective-permute-done.3 = bf16[32,32,4,256]{3,1,2,0:T(8,128)(2,1)} collective-permute-done((bf16[32,32,4,256]{3,1,2,0:T(8,128)(2,1)}, bf16[32,32,4,256]{3,1,2,0:T(8,128)(2,1)}, u32[]{:S(2)}, u32[]{:S(2)}) %collective-permute-start.3) | collective-permute-done | bytes 2097184 | tf_op jit(solution)/shard_map/ppermute | solution.py:15
  109.9 9.0 %fusion.7 = bf16[32,4,20,8,256]{4,3,2,1,0:T(8,128)(2,1)} fusion(s32[]{:T(128)S(6)} %select_n.68, bf16[32,32,4,256]{3,1,2,0:T(8,128)(2,1)} %collective-permute-done.4, bf16[32,96,4,256]{3,1,2,0:T(8,128)(2,1)S(1)} %bitcast.153, bf16[32,32,4,256]{3,1,2,0:T(8,128)(2,1)} %collective-permute-done.3), kind=kLoop, calls=%fused_computation.15 | loop fusion | flops 31457280 | bytes 20971524
  118.9 9.3 %copy.190 = bf16[32,4,20,8,256]{4,3,1,2,0:T(8,128)(2,1)} copy(bf16[32,4,20,8,256]{4,3,2,1,0:T(8,128)(2,1)} %fusion.7) | data formatting | bytes 20971520 | tf_op jit(solution)/shard_map/reshape | solution.py:177
  128.2 9.3 %convolution_convert_fusion.5 = bf16[32,96,1024]{2,1,0:T(8,128)(2,1)} fusion(bf16[32,160,1024]{2,1,0:T(8,128)(2,1)} %bitcast.142, bf16[32,96,160]{1,0,2:T(8,128)(2,1)} %get-tuple-element.53), kind=kOutput, calls=%fused_computation.57 | convolution fusion | flops 1009778688 | bytes 17760256 | tf_op jit(solution)/shard_map/wij,wjn->win/dot_general | solution.py:180
  137.6 10.7 %reshape.688 = bf16[32,384,256]{2,1,0:T(8,128)(2,1)} reshape(bf16[32,96,1024]{2,1,0:T(8,128)(2,1)} %convolution_convert_fusion.5) | data formatting | bytes 12582912 | tf_op jit(solution)/shard_map/reshape | solution.py:185
  148.3 9.3 %convolution_convert_fusion.6 = bf16[32,96,1024]{2,1,0:T(8,128)(2,1)} fusion(bf16[32,160,1024]{2,1,0:T(8,128)(2,1)} %bitcast.143, bf16[32,96,160]{1,0,2:T(8,128)(2,1)} %get-tuple-element.54), kind=kOutput, calls=%fused_computation.58 | convolution fusion | flops 1009778688 | bytes 17760256 | tf_op jit(solution)/shard_map/wij,wjn->win/dot_general | solution.py:180
  157.6 21.0 %reshape.687 = bf16[32,384,256]{2,1,0:T(8,128)(2,1)} reshape(bf16[32,96,1024]{2,1,0:T(8,128)(2,1)} %convolution_convert_fusion.6) | data formatting | bytes 12582912 | tf_op jit(solution)/shard_map/reshape | solution.py:185
  178.6 9.0 %convolution_convert_fusion.7 = bf16[32,96,1024]{2,1,0:T(8,128)(2,1)} fusion(bf16[32,160,1024]{2,1,0:T(8,128)(2,1)} %bitcast.144, bf16[32,96,160]{1,0,2:T(8,128)(2,1)S(1)} %get-tuple-element.55), kind=kOutput, calls=%fused_computation.59 | convolution fusion | flops 1009778688 | bytes 17760256 | tf_op jit(solution)/shard_map/wij,wjn->win/dot_general | solution.py:180
  187.6 10.8 %reshape.686 = bf16[32,384,256]{2,1,0:T(8,128)(2,1)} reshape(bf16[32,96,1024]{2,1,0:T(8,128)(2,1)} %convolution_convert_fusion.7) | data formatting | bytes 12582912 | tf_op jit(solution)/shard_map/reshape | solution.py:185
  198.4 9.0 %convolution_convert_fusion.4 = bf16[32,96,1024]{2,1,0:T(8,128)(2,1)} fusion(bf16[32,160,1024]{2,1,0:T(8,128)(2,1)} %bitcast.145, bf16[32,96,160]{1,0,2:T(8,128)(2,1)S(1)} %get-tuple-element.52), kind=kOutput, calls=%fused_computation.56 | convolution fusion | flops 1009778688 | bytes 17760256 | tf_op jit(solution)/shard_map/wij,wjn->win/dot_general | solution.py:180
  207.4 10.9 %reshape.689 = bf16[32,384,256]{2,1,0:T(8,128)(2,1)} reshape(bf16[32,96,1024]{2,1,0:T(8,128)(2,1)} %convolution_convert_fusion.4) | data formatting | bytes 12582912 | tf_op jit(solution)/shard_map/reshape | solution.py:185
  218.2 12.1 %fusion.24 = f32[32,384,256]{2,1,0:T(8,128)} fusion(bf16[32,384,256]{2,1,0:T(8,128)(2,1)} %reshape.688, bf16[32,256,256]{2,0,1:T(8,128)(2,1)} %get-tuple-element.41), kind=kOutput, calls=%fused_computation.48 | convolution fusion | flops 1610612736 | bytes 23068672 | tf_op jit(solution)/shard_map/wmc,wcd->wmd/dot_general | solution.py:183
  230.3 10.2 %fusion.27 = f32[32,384,256]{2,1,0:T(8,128)} fusion(bf16[32,384,256]{2,1,0:T(8,128)(2,1)S(1)} %bitcast.148, bf16[32,256,256]{2,0,1:T(8,128)(2,1)} %get-tuple-element.42), kind=kOutput, calls=%fused_computation.51 | convolution fusion | flops 1610612736 | bytes 23068672 | tf_op jit(solution)/shard_map/wmc,wcd->wmd/dot_general | solution.py:183
  248.6 22.9 %add_add_fusion.1 = f32[32,384,256]{2,1,0:T(8,128)} fusion(f32[32,384,256]{2,1,0:T(8,128)} %fusion.24, f32[32,384,256]{2,1,0:T(8,128)} %fusion.30, f32[32,384,256]{2,1,0:T(8,128)} %fusion.27, bf16[32,384,256]{2,1,0:T(8,128)(2,1)} %reshape.689, bf16[32,256,256]{2,0,1:T(8,128)(2,1)S(1)} %copy-done.5), kind=kOutput, calls=%fused_computation.13 | convolution fusion | flops 1620049920 | bytes 60817408 | tf_op jit(solution)/shard_map/wmc,wcd->wmd/dot_general | solution.py:183
  271.4 16.4 %copy.181 = f32[32,384,256]{2,0,1:T(8,128)} copy(f32[32,384,256]{2,1,0:T(8,128)} %add_add_fusion.1) | data formatting | bytes 25165824 | tf_op jit(solution)/shard_map/reshape | solution.py:190
  287.8 9.5 %fusion.5 = bf16[32,96,4,256]{3,0,2,1:T(8,128)(2,1)S(1)} fusion(f32[32,96,4,256]{3,0,2,1:T(8,128)} %bitcast.151, bf16[4,32,96,256]{3,2,1,0:T(8,128)(2,1)} %param.8, f32[96,4,256]{2,1,0:T(4,128)S(1)} %broadcast_multiply_fusion), kind=kLoop, calls=%fused_computation.11 | loop fusion | flops 12582912 | bytes 25559040 | tf_op jit(solution)/shard_map/convert_element_type | solution.py:197
  317.7 35.1 %collective-permute-done.5 = bf16[32,32,4,256]{3,0,2,1:T(8,128)(2,1)} collective-permute-done((bf16[32,32,4,256]{3,0,2,1:T(8,128)(2,1)}, bf16[32,32,4,256]{3,0,2,1:T(8,128)(2,1)}, u32[]{:S(2)}, u32[]{:S(2)}) %collective-permute-start.5) | collective-permute-done | bytes 2097184 | tf_op jit(solution)/shard_map/ppermute | solution.py:15
  352.8 9.1 %fusion.8 = bf16[32,160,4,256]{3,0,2,1:T(8,128)(2,1)} fusion(s32[]{:T(128)S(6)} %select_n.68, bf16[32,32,4,256]{3,0,2,1:T(8,128)(2,1)} %collective-permute-done.6, bf16[32,96,4,256]{3,0,2,1:T(8,128)(2,1)} %copy-done, bf16[32,32,4,256]{3,0,2,1:T(8,128)(2,1)} %collective-permute-done.5), kind=kLoop, calls=%fused_computation.16 | loop fusion | flops 10485760 | bytes 20971524 | tf_op jit(solution)/shard_map/add | solution.py:143
  361.9 18.3 %convolution_convert_fusion.2 = bf16[32,640,256]{2,1,0:T(8,128)(2,1)} fusion(bf16[32,640,256]{2,0,1:T(8,128)(2,1)} %bitcast.154, bf16[32,256,256]{2,0,1:T(8,128)(2,1)} %get-tuple-element.42), kind=kOutput, calls=%fused_computation.20 | convolution fusion | flops 2689597440 | bytes 25165824 | tf_op jit(solution)/shard_map/wmc,wdc->wmd/dot_general | solution.py:208
  380.2 24.4 %convolution_convert_fusion.3 = bf16[32,640,256]{2,1,0:T(8,128)(2,1)} fusion(bf16[32,640,256]{2,0,1:T(8,128)(2,1)} %bitcast.155, bf16[32,256,256]{2,0,1:T(8,128)(2,1)S(1)} %copy-done.4), kind=kOutput, calls=%fused_computation.21 | convolution fusion | flops 2689597440 | bytes 25165824 | tf_op jit(solution)/shard_map/wmc,wdc->wmd/dot_general | solution.py:208
  404.5 18.5 %convolution_convert_fusion = bf16[32,640,256]{2,1,0:T(8,128)(2,1)} fusion(bf16[32,640,256]{2,0,1:T(8,128)(2,1)} %bitcast.156, bf16[32,256,256]{2,0,1:T(8,128)(2,1)} %get-tuple-element.40), kind=kOutput, calls=%fused_computation.18 | convolution fusion | flops 2689597440 | bytes 25165824 | tf_op jit(solution)/shard_map/wmc,wdc->wmd/dot_general | solution.py:208
  423.0 24.5 %convolution_convert_fusion.1 = bf16[32,640,256]{2,1,0:T(8,128)(2,1)} fusion(bf16[32,640,256]{2,0,1:T(8,128)(2,1)} %bitcast.157, bf16[32,256,256]{2,0,1:T(8,128)(2,1)S(1)} %copy-done.2), kind=kOutput, calls=%fused_computation.19 | convolution fusion | flops 2689597440 | bytes 25165824 | tf_op jit(solution)/shard_map/wmc,wdc->wmd/dot_general | solution.py:208
  447.6 17.1 %reshape.693 = bf16[32,160,1024]{2,1,0:T(8,128)(2,1)} reshape(bf16[32,640,256]{2,1,0:T(8,128)(2,1)} %convolution_convert_fusion.2) | data formatting | bytes 20971520 | tf_op jit(solution)/shard_map/reshape | solution.py:214
  464.7 17.1 %reshape.692 = bf16[32,160,1024]{2,1,0:T(8,128)(2,1)} reshape(bf16[32,640,256]{2,1,0:T(8,128)(2,1)} %convolution_convert_fusion.3) | data formatting | bytes 20971520 | tf_op jit(solution)/shard_map/reshape | solution.py:214
  481.8 17.2 %reshape.695 = bf16[32,160,1024]{2,1,0:T(8,128)(2,1)} reshape(bf16[32,640,256]{2,1,0:T(8,128)(2,1)} %convolution_convert_fusion) | data formatting | bytes 20971520 | tf_op jit(solution)/shard_map/reshape | solution.py:214
  499.0 17.2 %reshape.694 = bf16[32,160,1024]{2,1,0:T(8,128)(2,1)} reshape(bf16[32,640,256]{2,1,0:T(8,128)(2,1)} %convolution_convert_fusion.1) | data formatting | bytes 20971520 | tf_op jit(solution)/shard_map/reshape | solution.py:214
  523.0 10.9 %fusion.52 = f32[32,96,1024]{2,1,0:T(8,128)} fusion(bf16[32,160,1024]{2,1,0:T(8,128)(2,1)} %reshape.692, bf16[32,96,160]{1,0,2:T(8,128)(2,1)S(1)} %copy-done.7), kind=kOutput, calls=%fused_computation.136 | convolution fusion | flops 1006632960 | bytes 24051712 | tf_op jit(solution)/shard_map/wij,wjn->win/dot_general | solution.py:211
  534.0 10.8 %fusion.48 = f32[32,96,1024]{2,1,0:T(8,128)} fusion(bf16[32,160,1024]{2,1,0:T(8,128)(2,1)} %reshape.694, bf16[32,96,160]{1,0,2:T(8,128)(2,1)S(1)} %copy-done.6), kind=kOutput, calls=%fused_computation.132 | convolution fusion | flops 1006632960 | bytes 24051712 | tf_op jit(solution)/shard_map/wij,wjn->win/dot_general | solution.py:211
  544.8 17.4 %add_add_fusion = f32[32,96,1024]{2,1,0:T(8,128)} fusion(f32[32,96,1024]{2,1,0:T(8,128)} %fusion.48, f32[32,96,1024]{2,1,0:T(8,128)} %fusion.52, f32[32,96,1024]{2,1,0:T(8,128)S(1)} %fusion.50, bf16[32,160,1024]{2,1,0:T(8,128)(2,1)} %reshape.695, bf16[32,96,160]{1,0,2:T(8,128)(2,1)S(1)} %get-tuple-element.48), kind=kOutput, calls=%fused_computation.12 | convolution fusion | flops 1016070144 | bytes 61800448 | tf_op jit(solution)/shard_map/wij,wjn->win/dot_general | solution.py:211
  562.2 11.1 %bitcast_multiply_fusion = f32[32,96,4,256]{3,1,2,0:T(8,128)} fusion(f32[32,12,4,8,256]{4,3,2,1,0:T(8,128)} %bitcast.146, f32[96]{0:T(128)S(1)} %copy-done.54), kind=kLoop, calls=%fused_computation.6 | loop fusion | flops 3145728 | bytes 25166208 | tf_op jit(solution)/shard_map/mul | solution.py:218
  576.2 14.7 %divide_add_fusion = (f32[32,96,256]{2,1,0:T(8,128)S(1)}, f32[32,96,256]{2,1,0:T(8,128)S(1)}, f32[32,96,256]{2,1,0:T(8,128)S(1)}, f32[32,96,256]{2,1,0:T(8,128)S...) fusion(f32[96,256]{1,0:T(8,128)S(1)} %copy-done.11, ...), kind=kLoop, calls=%fused_computation.76 | loop fusion | flops 90439680 | bytes 45711488 | tf_op jit(solution)/shard_map/transpose(jvp())/add_any | solution.py:55
  (225 shorter events, 150.0 us)
Async XLA Ops:
  0.0 7.6 %collective-permute-start = (f32[1,27648]{1,0:T(1,128)}, f32[1,27648]{1,0:T(1,128)S(1)}, u32[]{:S(2)}, u32[]{:S(2)}) collective-permute-start(f32[1,27648]{1,0:T(1,128)} %bitcast.160), channel_id=1, source_target_pairs={{0,16},{16,0},{32,48},{48,32},{64,80},{80,64},{96,112},{112,96},{1... | collective-permute-start | bytes 331784 | tf_op jit(solution)/shard_map/ppermute | solution.py:21
  7.6 44.5 %copy-start.53 = (f32[96]{0:T(128)}, f32[96]{0:T(128)S(1)}, u32[]{:S(2)}) copy-start(f32[96]{0:T(128)S(1)} %compare_convert_fusion) | copy-start | bytes 1156
  8.0 8.5 %collective-permute-start.1 = (f32[2,27648]{1,0:T(2,128)S(1)}, f32[2,27648]{1,0:T(2,128)S(1)}, u32[]{:S(2)}, u32[]{:S(2)}) collective-permute-start(f32[2,27648]{1,0:T(2,128)S(1)} %maximum_select_fusion.4), channel_id=1, source_target_pairs={{0,32},{16,48},{32,0},{48,16},{64,96},{80,112},{96,64},{112,80},{1... | collective-permute-start | bytes 663560 | tf_op jit(solution)/shard_map/ppermute | solution.py:21
  17.5 11.1 %collective-permute-start.2 = (f32[4,27648]{1,0:T(4,128)}, f32[4,27648]{1,0:T(4,128)}, u32[]{:S(2)}, u32[]{:S(2)}) collective-permute-start(f32[4,27648]{1,0:T(4,128)} %maximum_select_fusion.2), channel_id=1, source_target_pairs={{0,64},{16,80},{32,96},{48,112},{64,0},{80,16},{96,32},{112,48},{1... | collective-permute-start | bytes 1327112 | tf_op jit(solution)/shard_map/ppermute | solution.py:21
  19.1 26.6 %copy-start.51 = (f32[32]{0:T(128)}, f32[32]{0:T(128)S(1)}, u32[]{:S(2)}) copy-start(f32[32]{0:T(128)S(1)} %multiply_add_fusion.9) | copy-start | bytes 388
  33.9 18.1 %copy-start.32 = (f32[1,8,12,256]{3,2,1,0:T(8,128)}, f32[1,8,12,256]{3,2,1,0:T(8,128)S(1)}, u32[]{:S(2)}) copy-start(f32[1,8,12,256]{3,2,1,0:T(8,128)S(1)} %get-tuple-element.64) | copy-start | bytes 294916
  33.9 18.1 %copy-start.34 = (f32[1,8,12,256]{3,2,1,0:T(8,128)}, f32[1,8,12,256]{3,2,1,0:T(8,128)S(1)}, u32[]{:S(2)}) copy-start(f32[1,8,12,256]{3,2,1,0:T(8,128)S(1)} %get-tuple-element.67) | copy-start | bytes 294916
  34.0 18.1 %copy-start.8 = (f32[96,256]{1,0:T(8,128)}, f32[96,256]{1,0:T(8,128)S(1)}, u32[]{:S(2)}) copy-start(f32[96,256]{1,0:T(8,128)S(1)} %add.435) | copy-start | bytes 294916
  35.1 17.0 %copy-start.10 = (f32[96,256]{1,0:T(8,128)}, f32[96,256]{1,0:T(8,128)S(1)}, u32[]{:S(2)}) copy-start(f32[96,256]{1,0:T(8,128)S(1)} %add.437) | copy-start | bytes 294916
  35.1 17.0 %copy-start.18 = (f32[96,256]{1,0:T(8,128)}, f32[96,256]{1,0:T(8,128)S(1)}, u32[]{:S(2)}) copy-start(f32[96,256]{1,0:T(8,128)S(1)} %cos.46) | copy-start | bytes 294916
  38.0 14.1 %copy-start.12 = (f32[96,256]{1,0:T(8,128)}, f32[96,256]{1,0:T(8,128)S(1)}, u32[]{:S(2)}) copy-start(f32[96,256]{1,0:T(8,128)S(1)} %add.427) | copy-start | bytes 294916
  39.0 13.1 %copy-start.14 = (f32[96,256]{1,0:T(8,128)}, f32[96,256]{1,0:T(8,128)S(1)}, u32[]{:S(2)}) copy-start(f32[96,256]{1,0:T(8,128)S(1)} %add.433) | copy-start | bytes 294916
  39.9 12.2 %copy-start.20 = (f32[96,256]{1,0:T(8,128)}, f32[96,256]{1,0:T(8,128)S(1)}, u32[]{:S(2)}) copy-start(f32[96,256]{1,0:T(8,128)S(1)} %mul.1331) | copy-start | bytes 294916
  54.3 11.3 %copy-start.46 = (f32[96,256]{1,0:T(8,128)S(1)}, f32[96,256]{1,0:T(8,128)}, u32[]{:S(2)}) copy-start(f32[96,256]{1,0:T(8,128)} %convert_multiply_fusion) | copy-start | bytes 294916
  54.3 11.3 %copy-start.55 = (f32[4]{0:T(128)S(1)}, f32[4]{0:T(128)}, u32[]{:S(2)}) copy-start(f32[4]{0:T(128)} %constant.119) | copy-start | bytes 52
  54.3 11.4 %copy-start.56 = (bf16[32,4,65]{2,1,0:T(4,128)(2,1)S(1)}, bf16[32,4,65]{2,1,0:T(4,128)(2,1)}, u32[]{:S(2)}) copy-start(bf16[32,4,65]{2,1,0:T(4,128)(2,1)} %param.10) | copy-start | bytes 49924
  58.2 51.6 %collective-permute-start.3 = (bf16[32,32,4,256]{3,1,2,0:T(8,128)(2,1)}, bf16[32,32,4,256]{3,1,2,0:T(8,128)(2,1)}, u32[]{:S(2)}, u32[]{:S(2)}) collective-permute-start(bf16[32,32,4,256]{3,1,2,0:T(8,128)(2,1)} %get-tuple-element.46), channel_id=1, source_target_pairs={{0,1},{1,2},{2,3},{3,4},{4,5},{5,6},{6,7},{7,8},{8,9},{9,10},{10,1... | collective-permute-start | bytes 6291464 | tf_op jit(solution)/shard_map/ppermute | solution.py:15
  60.1 49.7 %collective-permute-start.4 = (bf16[32,32,4,256]{3,1,2,0:T(8,128)(2,1)}, bf16[32,32,4,256]{3,1,2,0:T(8,128)(2,1)}, u32[]{:S(2)}, u32[]{:S(2)}) collective-permute-start(bf16[32,32,4,256]{3,1,2,0:T(8,128)(2,1)} %get-tuple-element.47), channel_id=1, source_target_pairs={{1,0},{2,1},{3,2},{4,3},{5,4},{6,5},{7,6},{8,7},{9,8},{10,9},{11,1... | collective-permute-start | bytes 6291464 | tf_op jit(solution)/shard_map/ppermute | solution.py:15
  65.7 44.1 %slice-start.4 = ((s8[6291456]{0:T(1024)(128)(4,1)}), s8[2097152]{0:T(1024)(128)(4,1)S(1)}, s32[]{:S(2)}) async-start(s8[6291456]{0:T(1024)(128)(4,1)} %bitcast.152), calls=%async_computation.4 | async-start | bytes 4194304
  74.1 35.7 %slice-start.5 = ((s8[6291456]{0:T(1024)(128)(4,1)}), s8[4194304]{0:T(1024)(128)(4,1)S(1)}, s32[]{:S(2)}) async-start(s8[6291456]{0:T(1024)(128)(4,1)} %bitcast.152), calls=%async_computation.5 | async-start | bytes 8388608
  207.4 22.9 %slice-start = ((s8[6291456]{0:T(1024)(128)(4,1)}), s8[2097152]{0:T(1024)(128)(4,1)S(1)}, s32[]{:S(2)}) async-start(s8[6291456]{0:T(1024)(128)(4,1)} %bitcast.147), calls=%async_computation | async-start | bytes 4194304
  218.2 12.1 %slice-start.1 = ((s8[6291456]{0:T(1024)(128)(4,1)}), s8[4194304]{0:T(1024)(128)(4,1)S(1)}, s32[]{:S(2)}) async-start(s8[6291456]{0:T(1024)(128)(4,1)} %bitcast.147), calls=%async_computation.1 | async-start | bytes 8388608
  218.2 22.3 %slice-start.2 = ((s8[6291456]{0:T(1024)(128)(4,1)}), s8[4194304]{0:T(1024)(128)(4,1)S(1)}, s32[]{:S(2)}) async-start(s8[6291456]{0:T(1024)(128)(4,1)} %bitcast.149), calls=%async_computation.2 | async-start | bytes 8388608
  301.2 51.6 %collective-permute-start.5 = (bf16[32,32,4,256]{3,0,2,1:T(8,128)(2,1)}, bf16[32,32,4,256]{3,0,2,1:T(8,128)(2,1)}, u32[]{:S(2)}, u32[]{:S(2)}) collective-permute-start(bf16[32,32,4,256]{3,0,2,1:T(8,128)(2,1)} %get-tuple-element.44), channel_id=1, source_target_pairs={{0,1},{1,2},{2,3},{3,4},{4,5},{5,6},{6,7},{7,8},{8,9},{9,10},{10,1... | collective-permute-start | bytes 6291464 | tf_op jit(solution)/shard_map/ppermute | solution.py:15
  303.1 49.7 %collective-permute-start.6 = (bf16[32,32,4,256]{3,0,2,1:T(8,128)(2,1)}, bf16[32,32,4,256]{3,0,2,1:T(8,128)(2,1)}, u32[]{:S(2)}, u32[]{:S(2)}) collective-permute-start(bf16[32,32,4,256]{3,0,2,1:T(8,128)(2,1)} %get-tuple-element.45), channel_id=1, source_target_pairs={{1,0},{2,1},{3,2},{4,3},{5,4},{6,5},{7,6},{8,7},{9,8},{10,9},{11,1... | collective-permute-start | bytes 6291464 | tf_op jit(solution)/shard_map/ppermute | solution.py:15
  361.9 18.3 %copy-start.4 = (bf16[32,256,256]{2,0,1:T(8,128)(2,1)S(1)}, bf16[32,256,256]{2,0,1:T(8,128)(2,1)}, u32[]{:S(2)}) copy-start(bf16[32,256,256]{2,0,1:T(8,128)(2,1)} %get-tuple-element.43) | copy-start | bytes 12582916
  404.5 18.5 %copy-start.2 = (bf16[32,256,256]{2,0,1:T(8,128)(2,1)S(1)}, bf16[32,256,256]{2,0,1:T(8,128)(2,1)}, u32[]{:S(2)}) copy-start(bf16[32,256,256]{2,0,1:T(8,128)(2,1)} %get-tuple-element.41) | copy-start | bytes 12582916
  523.0 10.9 %copy-start.6 = (bf16[32,96,160]{1,0,2:T(8,128)(2,1)S(1)}, bf16[32,96,160]{1,0,2:T(8,128)(2,1)}, u32[]{:S(2)}) copy-start(bf16[32,96,160]{1,0,2:T(8,128)(2,1)} %get-tuple-element.49) | copy-start | bytes 2949124
  544.8 17.4 %copy-start.54 = (f32[96]{0:T(128)S(1)}, f32[96]{0:T(128)}, u32[]{:S(2)}) copy-start(f32[96]{0:T(128)} %copy-done.53) | copy-start | bytes 1156
  607.2 8.4 %collective-permute-start.7 = (f32[4,9,12,256]{3,0,2,1:T(4,128)S(1)}, f32[4,9,12,256]{3,0,2,1:T(4,128)S(1)}, u32[]{:S(2)}, u32[]{:S(2)}) collective-permute-start(f32[4,9,12,256]{3,0,2,1:T(4,128)S(1)} %copy.177), channel_id=1, source_target_pairs={{0,64},{16,80},{32,96},{48,112},{64,0},{80,16},{96,32},{112,48},{1... | collective-permute-start | bytes 1327112 | tf_op jit(solution)/shard_map/ppermute | solution.py:21
  616.0 8.3 %collective-permute-start.8 = (f32[2,9,12,256]{3,2,0,1:T(8,128)S(1)}, f32[2,9,12,256]{3,2,0,1:T(8,128)S(1)}, u32[]{:S(2)}, u32[]{:S(2)}) collective-permute-start(f32[2,9,12,256]{3,2,0,1:T(8,128)S(1)} %constant_dynamic-slice_fusion.1), channel_id=1, source_target_pairs={{0,32},{16,48},{32,0},{48,16},{64,96},{80,112},{96,64},{112,80},{1... | collective-permute-start | bytes 663560 | tf_op jit(solution)/shard_map/ppermute | solution.py:21
  624.4 5.2 collective-permute-start.9
  (41 other events, 195.8 us)
